TPU v7x, 256 devices: a whole 4x4x8 slice. The times are simulated.
256 devices in a mesh: wave: 64 (over z, y, core), lev: 4 (over x).
Axes of the slice: x: 4, y: 4, z: 8, core: 2. Of those that a mesh axis runs over, the one named last changes fastest.
Arguments:
- coefficients: bfloat16 [640, 2, 128, 640], P('wave', None, 'lev'), may hold values from -0.1796875 to 0.1796875
- legendre: bfloat16 [640, 2, 640, 512], P('wave'), may hold values from -0.25 to 0.25
- pair_wave: int32 [640], replicated, may hold values from 0 to 639, each once
- row_points: int32 [512], replicated, may hold values from 20 to 5136, as said below
- layer_logpressure_factor: float32 [16], replicated, may hold values from 0.05 to 0.5
Outputs:
- physical_space_values: bfloat16 [1024, 64, 5248], P('wave', 'lev')
- geopotential: bfloat16 [1024, 16, 5248], P('wave', 'lev')
Inputs may be any that keep to these rules, and one draw needn't show every extreme that they name: Pair q holds zonal wavenumbers pair_wave[q] and 1279 - pair_wave[q]; each value appears once. `row_points`: the northern rows from the pole toward the equator: 16 + 4 j points for distinct octahedral rows j of 1 to 1280, strictly rising; the last row is j = 1280.
All inputs are finite; a program needn't handle non-finite values.
Results may differ from a plain program's by a relative error of at most 0.0062.
Values may be sent and summed in bfloat16 or wider, within the bound.
No kernel may reach another device: no remote copies, remote signals or barrier semaphores. Data moves between devices by JAX's collectives and lax.ppermute only.
A program may use at most 128 MiB of HBM per device.

v0:
```python
import jax
import jax.numpy as jnp
from jax import lax
from jax.sharding import PartitionSpec as P
from jax.experimental import pallas as pl
from jax.experimental.pallas import tpu as pltpu

TRUNC = 1279
QUANTITY_COUNT = 4
LCAP = 5248
BLOCK = 128
BLOCKS = LCAP // BLOCK
DEPTH = 48

two_pi = 6.283185307179586


def pair_masks(low_waves, pack_width):
    parity = jnp.arange(2, dtype=jnp.int32)
    low_count = (TRUNC - low_waves[:, None] - parity[None, :]) // 2 + 1
    high_count = (low_waves[:, None] - parity[None, :]) // 2 + 1
    pack_index = jnp.arange(pack_width, dtype=jnp.int32)[None, None, :]
    low_mask = pack_index < low_count[:, :, None]
    high_mask = (pack_index >= low_count[:, :, None]) & (
        pack_index < (low_count + high_count)[:, :, None]
    )
    return jnp.stack([low_mask, high_mask], axis=2)


def residue(j, points):
    q = jnp.floor(j.astype(jnp.float32) / points.astype(jnp.float32)).astype(jnp.int32)
    r = j - q * points
    r = jnp.where(r < 0, r + points, r)
    return jnp.where(r >= points, r - points, r)


def phase(waves, steps, points):
    j = waves * steps
    rem = residue(j, points)
    angle = rem.astype(jnp.float32) * (jnp.float32(two_pi) / points.astype(jnp.float32))
    return jnp.cos(angle), jnp.sin(angle)


def times(a, b):
    return a[0] * b[0] - a[1] * b[1], a[1] * b[0] + a[0] * b[1]


def tables(wave_numbers, lengths):
    w = wave_numbers[None, None, :]
    pts = lengths[:, None, None]
    low = phase(w, jnp.arange(16, dtype=jnp.int32)[None, :, None], pts)
    high = phase(w, 16 * jnp.arange(8, dtype=jnp.int32)[None, :, None], pts)
    near = phase(w, BLOCK * jnp.arange(8, dtype=jnp.int32)[None, :, None], pts)
    far = phase(w, 8 * BLOCK * jnp.arange(8, dtype=jnp.int32)[None, :, None], pts)
    wave_limit = jnp.minimum(TRUNC, (lengths - 1) // 2)
    keep = (wave_numbers[None, :] <= wave_limit[:, None]).astype(jnp.float32)[:, None, :]
    return jnp.concatenate(
        [low[0], low[1], high[0], high[1], near[0] * keep, near[1] * keep, far[0], far[1]], axis=1
    )


def expand(ph_ref, base_ref, tcos_ref, tsin_ref):
    slots = ph_ref.shape[2]
    p0c = ph_ref[0, 0:16, :]
    p0s = ph_ref[0, 16:32, :]
    for k1 in range(8):
        a = ph_ref[0, 32 + k1:33 + k1, :]
        b = ph_ref[0, 40 + k1:41 + k1, :]
        rows = slice(16 * k1, 16 * (k1 + 1))
        base_ref[rows, 0:slots] = (a * p0c - b * p0s).astype(jnp.bfloat16)
        base_ref[rows, slots:2 * slots] = (-(b * p0c + a * p0s)).astype(jnp.bfloat16)
    q0c = ph_ref[0, 48:56, :]
    q0s = ph_ref[0, 56:64, :]
    for b1 in range(6):
        a = ph_ref[0, 64 + b1:65 + b1, :]
        b = ph_ref[0, 72 + b1:73 + b1, :]
        rows = slice(8 * b1, 8 * (b1 + 1))
        tcos_ref[rows, :] = a * q0c - b * q0s
        tsin_ref[rows, :] = b * q0c + a * q0s


def main_kernel(lengths_ref, rowmap_ref, f_ref, ph_ref, out_ref, tw_ref, base_ref, cos_ref, sin_ref):
    expand(ph_ref, base_ref, cos_ref, sin_ref)
    r = pl.program_id(0)
    points = lengths_ref[r]
    fields = out_ref.shape[1]
    slots = f_ref.shape[2]
    real_part = f_ref[0, 0:fields, :]
    imag_part = f_ref[0, fields:2 * fields, :]
    for b in range(BLOCKS):
        c = cos_ref[b:b + 1, :]
        s = sin_ref[b:b + 1, :]
        rows = slice(fields * b, fields * (b + 1))
        tw_ref[rows, 0:slots] = (real_part * c - imag_part * s).astype(jnp.bfloat16)
        tw_ref[rows, slots:2 * slots] = (real_part * s + imag_part * c).astype(jnp.bfloat16)
    values = lax.dot_general(tw_ref[...], base_ref[...], (((1,), (1,)), ((), ())),
                             preferred_element_type=jnp.float32)
    lane = lax.broadcasted_iota(jnp.int32, (fields, BLOCK), 1)
    for b in range(BLOCKS):
        v = values[fields * b:fields * (b + 1), :]
        v = jnp.where(lane + BLOCK * b < points, v, 0.0)
        out_ref[0, :, BLOCK * b:BLOCK * (b + 1)] = v.astype(jnp.bfloat16)


def heat_kernel(lengths_ref, rowmap_ref, f_ref, ph_ref, out_ref, tw_ref, base_ref, cos_ref, sin_ref):
    expand(ph_ref, base_ref, cos_ref, sin_ref)
    slots = f_ref.shape[2]
    depth = cos_ref.shape[0]
    fields = f_ref.shape[1] // 2
    c = cos_ref[...]
    s = sin_ref[...]
    for f in range(fields):
        re = f_ref[0, f:f + 1, :]
        im = f_ref[0, fields + f:fields + f + 1, :]
        rows = slice(depth * f, depth * (f + 1))
        tw_ref[rows, 0:slots] = (re * c - im * s).astype(jnp.bfloat16)
        tw_ref[rows, slots:2 * slots] = (re * s + im * c).astype(jnp.bfloat16)
    out_ref[0] = lax.dot_general(tw_ref[...], base_ref[...], (((1,), (1,)), ((), ())),
                                 preferred_element_type=jnp.float32)


def synth(kernel, fourier, ph, lengths, rowmap, out_rows, out_cols, out_dtype, tw_rows):
    rows, cols, slots = fourier.shape
    grid_spec = pltpu.PrefetchScalarGridSpec(
        num_scalar_prefetch=2,
        grid=(rows,),
        in_specs=[
            pl.BlockSpec((1, cols, slots), lambda r, n, m: (m[r], 0, 0)),
            pl.BlockSpec((1, ph.shape[1], slots), lambda r, n, m: (r, 0, 0)),
        ],
        out_specs=pl.BlockSpec((1, out_rows, out_cols), lambda r, n, m: (r, 0, 0)),
        scratch_shapes=[
            pltpu.VMEM((tw_rows, 2 * slots), jnp.bfloat16),
            pltpu.VMEM((BLOCK, 2 * slots), jnp.bfloat16),
            pltpu.VMEM((DEPTH, slots), jnp.float32),
            pltpu.VMEM((DEPTH, slots), jnp.float32),
        ],
    )
    return pl.pallas_call(
        kernel,
        grid_spec=grid_spec,
        out_shape=jax.ShapeDtypeStruct((rows, out_rows, out_cols), out_dtype),
        compiler_params=pltpu.CompilerParams(dimension_semantics=("arbitrary",)),
    )(lengths, rowmap, fourier, ph)


def local(coefficients, legendre, pair_wave, row_points, layer_logpressure_factor):
    wave_count = lax.axis_size("wave")
    wave_rank = lax.axis_index("wave")
    pair_local, _, cols, pack_width = coefficients.shape
    fields = cols // 2
    half_rows = legendre.shape[3]
    all_rows = 2 * half_rows
    band_rows = all_rows // wave_count
    half_bands = half_rows // band_rows
    my_pairs = lax.dynamic_slice_in_dim(pair_wave, wave_rank * pair_local, pair_local)
    selection = pair_masks(my_pairs, pack_width).astype(jnp.bfloat16)
    coef = coefficients.reshape(pair_local, 2, fields, 2, pack_width).transpose(0, 1, 3, 2, 4)
    coef = coef.reshape(pair_local, 2, cols, pack_width)
    selected = coef[:, :, None, :, :] * selection[:, :, :, None, :]
    signs = jnp.array([[1.0, 1.0], [1.0, -1.0]], jnp.bfloat16)
    lhs = signs[None, :, :, None, None, None] * selected[:, None]
    sums = jnp.einsum("qaehci,qeit->qahct", lhs, legendre, preferred_element_type=jnp.float32)
    sums = sums.reshape(pair_local, 2, 2, cols, half_bands, band_rows)
    north = sums[:, 0]
    south = jnp.flip(sums[:, 1], 3)
    bands = jnp.concatenate([north, south], 3)
    send = bands.transpose(3, 0, 1, 4, 2).reshape(wave_count, pair_local * 2, band_rows * cols)
    got = lax.all_to_all(send, "wave", 0, 0, tiled=True)
    slots = got.shape[0] * got.shape[1]
    fourier = got.reshape(slots, band_rows * cols).T.reshape(band_rows, cols, slots)
    south_side = (wave_rank >= half_bands).astype(jnp.int32)
    local_rows = jnp.arange(band_rows, dtype=jnp.int32)
    rowmap = local_rows + south_side * (band_rows - 1 - 2 * local_rows)

    wave_numbers = jnp.stack([pair_wave, TRUNC - pair_wave], axis=1).reshape(-1)
    points_all = jnp.concatenate([row_points, jnp.flip(row_points)])
    lengths = lax.dynamic_slice_in_dim(points_all, wave_rank * band_rows, band_rows)
    ph = tables(wave_numbers, lengths)
    heat_cols = fourier.reshape(band_rows, 2, fields // QUANTITY_COUNT, QUANTITY_COUNT, slots)[:, :, :, 0]
    heat_cols = heat_cols.reshape(band_rows, 2 * fields // QUANTITY_COUNT, slots)
    heat_fields = fields // QUANTITY_COUNT
    depth = DEPTH
    raw = synth(heat_kernel, heat_cols, ph, lengths, rowmap,
                heat_fields * depth, BLOCK, jnp.float32, heat_fields * depth)
    raw = raw.reshape(band_rows, heat_fields, depth, BLOCK)[:, :, :BLOCKS].reshape(band_rows, heat_fields, LCAP)
    position = jnp.arange(LCAP, dtype=jnp.int32)
    raw = jnp.where(position[None, None, :] < lengths[:, None, None], raw, 0.0)
    heat_state_values = raw.astype(jnp.bfloat16).astype(jnp.float32)
    values = synth(main_kernel, fourier, ph, lengths, rowmap,
                   fields, LCAP, jnp.bfloat16, fields * BLOCKS)

    device_layers = heat_state_values.shape[1]
    lev_rank = lax.axis_index("lev")
    layer_depth_factor = lax.dynamic_slice_in_dim(
        layer_logpressure_factor, lev_rank * device_layers, device_layers
    )
    scaled_heat_values = heat_state_values * layer_depth_factor[None, :, None]
    partial_totals = jnp.flip(jnp.cumsum(jnp.flip(scaled_heat_values, 1), axis=1), 1)
    everything = lax.all_gather(partial_totals[:, 0, :], "lev")
    lev_count = everything.shape[0]
    below = (jnp.arange(lev_count) > lev_rank).astype(jnp.float32)[:, None, None]
    deeper = jnp.sum(everything * below, axis=0)
    geopotential = (partial_totals + deeper[:, None, :]).astype(jnp.bfloat16)
    return (values, geopotential)


def solution(mesh):
    return jax.shard_map(
        local,
        mesh=mesh,
        in_specs=(P("wave", None, "lev", None), P("wave", None, None, None), P(), P(), P()),
        out_specs=(P("wave", "lev", None), P("wave", "lev", None)),
        check_vma=False,
    )
```

profile of v0, /device:TPU:2, one launch (start us, length us, event | category | flops | bytes accessed | tf_op | source)
XLA Modules:
  0.0 209.9 jit_solution(3349357272749609079)
XLA Ops:
  7.2 1.9 copy.29
  9.1 0.1 copy.30
  9.2 0.1 broadcast_subtract_fusion.1
  9.3 0.1 fusion.31
  9.4 0.1 iota_compare_fusion.1
  9.5 0.1 add_convert_fusion.1
  9.6 0.2 broadcast_multiply_fusion
  9.8 0.0 copy-done.5
  9.8 9.8 %fusion = f32[10,2,2,32,512,1]{3,4,5,2,1,0:T(8,128)S(1)} fusion(bf16[10,2,640,512]{3,2,1,0:T(8,128)(2,1)} %param.7, bf16[10,2,2,32,640]{4,3,1,2,0:T(8,128)(2,1)S(1)} %broadcast_multiply_fusion, bf16[2,2]{1,0:T(2,128)(2,1)S(1)} %copy-done.5), kind=kOutput, calls=%fused_computation | convolution fusion | flops 1679360000 | bytes 17367048 | tf_op jit(solution)/shard_map/qaehci,qeit->qahct/dot_general | solution.py:163
  19.7 4.7 %slice_bitcast_fusion.1 = (f32[10,2,32,32,16]{2,4,3,1,0:T(8,128)}, f32[10,2,32,32,16]{2,4,3,1,0:T(8,128)}) fusion(f32[10,2,2,32,32,16]{3,5,4,2,1,0:T(8,128)S(1)} %bitcast.28), kind=kLoop, calls=%fused_computation.4 | loop fusion | bytes 5242880 | tf_op jit(solution)/shard_map/squeeze | solution.py:165
  24.4 5.2 %rev.16 = f32[10,2,32,32,16]{2,4,3,1,0:T(8,128)} reverse(f32[10,2,32,32,16]{2,4,3,1,0:T(8,128)} %get-tuple-element.13), dimensions={3} | reverse | bytes 2621440 | tf_op jit(solution)/shard_map/jit(_flip)/rev | solution.py:166
  29.6 9.1 %maximum_bitcast_fusion = f32[64,10,2,16,32]{4,3,0,2,1:T(8,128)} fusion(f32[10,2,32,32,16]{2,4,3,1,0:T(8,128)} %rev.16, f32[10,2,32,32,16]{2,4,3,1,0:T(8,128)} %get-tuple-element.12), kind=kLoop, calls=%fused_computation.2 | loop fusion | flops 655360 | bytes 5242880 | tf_op jit(solution)/shard_map/transpose | solution.py:168
  38.7 9.5 %copy.33 = f32[64,10,2,16,32]{0,4,3,2,1:T(8,128)} copy(f32[64,10,2,16,32]{4,3,0,2,1:T(8,128)} %maximum_bitcast_fusion) | data formatting | bytes 5242880 | tf_op jit(solution)/shard_map/transpose | solution.py:168
  48.2 5.9 %copy.34 = f32[64,20,512]{2,1,0:T(8,128)} copy(f32[64,20,512]{0,2,1:T(8,128)} %bitcast.27) | data formatting | bytes 5242880 | tf_op jit(solution)/shard_map/reshape | solution.py:168
  54.0 12.2 %all-to-all-start = ((f32[64,20,512]{2,1,0:T(8,128)}), f32[64,20,512]{2,1,0:T(8,128)S(1)}, u32[]{:S(2)}, u32[]{:S(2)}) async-start(f32[64,20,512]{2,1,0:T(8,128)} %copy.34), calls=%async_computation | async-start | bytes 6291456 | tf_op jit(solution)/shard_map/all_to_all | solution.py:169
  66.3 0.1 rev.15
  66.4 0.5 fusion.39
  67.1 0.2 copy.36
  67.3 0.2 mul.254
  67.5 0.1 dynamic_slice.11
  67.6 0.1 broadcast_multiply_fusion.1
  67.7 6.0 %cosine_dynamic-update-slice_fusion = f32[16,80,1280]{2,1,0:T(8,128)} fusion(f32[16]{0:T(128)S(1)} %broadcast_divide_fusion, s32[16]{0:T(128)S(1)} %get-tuple-element.9.lengths_ref, f32[16]{0:T(128)S(1)} %convert_element_type.103, f32[16,1280]{1,0:T(8,128)S(1)} %get-tuple-element.25, s32[16,1280]{1,0:T(8,128)S(1)} %get-tuple-element.24), kind=kLoop, calls=%fused_computation.28 | loop fusion | flops 4259839 | bytes 1474752
  73.7 0.1 compare_convert_fusion
  73.8 5.9 %sine_dynamic-update-slice_fusion = f32[16,80,1280]{2,1,0:T(8,128)} fusion(f32[16,80,1280]{2,1,0:T(8,128)} %cosine_dynamic-update-slice_fusion, f32[16]{0:T(128)S(1)} %broadcast_divide_fusion, s32[16]{0:T(128)S(1)} %get-tuple-element.9.lengths_ref, f32[16]{0:T(128)S(1)} %convert_element_type.103, f32[16,1280]{1,0:T(8,128)S(1)} %get-tuple-element.25, ...), kind=kLoop, calls=%fused_computation.27 | loop fusion | flops 4259840 | bytes 1474752
  79.7 3.3 %cosine_dynamic-update-slice_fusion.2 = f32[16,80,1280]{2,1,0:T(8,128)} fusion(f32[16,80,1280]{2,1,0:T(8,128)} %sine_dynamic-update-slice_fusion, f32[16]{0:T(128)S(1)} %broadcast_divide_fusion, s32[16]{0:T(128)S(1)} %get-tuple-element.9.lengths_ref, f32[16]{0:T(128)S(1)} %convert_element_type.103, f32[8,1280]{1,0:T(8,128)S(1)} %get-tuple-element.22, ...), kind=kLoop, calls=%fused_computation.54 | loop fusion | flops 2129920 | bytes 737472
  83.0 3.3 %sine_dynamic-update-slice_fusion.2 = f32[16,80,1280]{2,1,0:T(8,128)} fusion(f32[16,80,1280]{2,1,0:T(8,128)} %cosine_dynamic-update-slice_fusion.2, f32[16]{0:T(128)S(1)} %broadcast_divide_fusion, s32[16]{0:T(128)S(1)} %get-tuple-element.9.lengths_ref, f32[16]{0:T(128)S(1)} %convert_element_type.103, f32[8,1280]{1,0:T(8,128)S(1)} %get-tuple-element.22, ...), kind=kLoop, calls=%fused_computation.53 | loop fusion | flops 2129920 | bytes 737472
  86.3 3.3 %multiply_dynamic-update-slice_fusion.1 = f32[16,80,1280]{2,1,0:T(8,128)} fusion(f32[16,80,1280]{2,1,0:T(8,128)} %sine_dynamic-update-slice_fusion.2, f32[16,1280]{1,0:T(8,128)S(1)} %compare_convert_fusion, f32[16]{0:T(128)S(1)} %broadcast_divide_fusion, s32[16]{0:T(128)S(1)} %get-tuple-element.9.lengths_ref, f32[16]{0:T(128)S(1)} %convert_element_type.103, ...), kind=kLoop, calls=%fused_computation.52 | loop fusion | flops 2293760 | bytes 819392
  89.6 3.3 %multiply_dynamic-update-slice_fusion = f32[16,80,1280]{2,1,0:T(8,128)} fusion(f32[16,80,1280]{2,1,0:T(8,128)} %multiply_dynamic-update-slice_fusion.1, f32[16,1280]{1,0:T(8,128)S(1)} %compare_convert_fusion, f32[16]{0:T(128)S(1)} %broadcast_divide_fusion, s32[16]{0:T(128)S(1)} %get-tuple-element.9.lengths_ref, f32[16]{0:T(128)S(1)} %convert_element_type.103, ...), kind=kLoop, calls=%fused_computation.51 | loop fusion | flops 2293760 | bytes 819392
  92.9 3.3 %cosine_dynamic-update-slice_fusion.1 = f32[16,80,1280]{2,1,0:T(8,128)} fusion(f32[16,80,1280]{2,1,0:T(8,128)} %multiply_dynamic-update-slice_fusion, f32[16]{0:T(128)S(1)} %broadcast_divide_fusion, s32[16]{0:T(128)S(1)} %get-tuple-element.9.lengths_ref, f32[16]{0:T(128)S(1)} %convert_element_type.103, f32[8,1280]{1,0:T(8,128)S(1)} %get-tuple-element.15, ...), kind=kLoop, calls=%fused_computation.50 | loop fusion | flops 2129920 | bytes 737472
  96.2 3.3 %sine_dynamic-update-slice_fusion.1.ph_ref = f32[16,80,1280]{2,1,0:T(8,128)} fusion(f32[16,80,1280]{2,1,0:T(8,128)} %cosine_dynamic-update-slice_fusion.1, f32[16]{0:T(128)S(1)} %broadcast_divide_fusion, s32[16]{0:T(128)S(1)} %get-tuple-element.9.lengths_ref, f32[16]{0:T(128)S(1)} %convert_element_type.103, f32[8,1280]{1,0:T(8,128)S(1)} %get-tuple-element.15, ...), kind=kLoop, calls=%fused_computation.49 | loop fusion | flops 2129920 | bytes 737472 | tf_op jit(solution)/shard_map/concatenate | solution.py:57
  99.5 0.1 iota_compare_fusion
  99.6 40.5 %all-to-all-done = f32[64,20,512]{2,1,0:T(8,128)S(1)} async-done(((f32[64,20,512]{2,1,0:T(8,128)}), f32[64,20,512]{2,1,0:T(8,128)S(1)}, u32[]{:S(2)}, u32[]{:S(2)}) %all-to-all-start) | async-done | bytes 2621472 | tf_op jit(solution)/shard_map/all_to_all | solution.py:169
  140.1 1.6 reshape.477
  141.8 2.1 %copy.35 = f32[512,1280]{1,0:T(8,128)S(1)} copy(f32[512,1280]{0,1:T(8,128)} %bitcast.29) | data formatting | bytes 5242880 | tf_op jit(solution)/shard_map/transpose | solution.py:171
  143.9 2.3 %reshape_reshape.3 = f32[16,2,4,4,1280]{4,3,2,1,0:T(4,128)} reshape(f32[512,1280]{1,0:T(8,128)S(1)} %copy.35) | data formatting | bytes 5242880 | tf_op jit(solution)/shard_map/reshape;reshape | solution.py:180
  146.3 3.6 %slice_reduce_fusion = f32[16,2,4,1280]{3,2,1,0:T(4,128)S(1)} fusion(f32[16,2,4,4,1280]{4,3,2,1,0:T(4,128)} %reshape_reshape.3), kind=kLoop, calls=%fused_computation.48 | loop fusion | bytes 1310720 | tf_op jit(solution)/shard_map/slice | solution.py:180
  149.9 1.1 reshape_squeeze.3.f_ref
  150.9 15.8 %shard_map.78 = f32[16,192,128]{2,1,0:T(8,128)} custom-call(s32[16]{0:T(128)} %copy-done.1, s32[16]{0:T(128)} %get-tuple-element.32.rowmap_ref, f32[16,8,1280]{2,1,0:T(8,128)} %reshape_squeeze.3.f_ref, f32[16,80,1280]{2,1,0:T(8,128)} %sine_dynamic-update-slice_fusion.1.ph_ref), custom_call_target="tpu_custom_call" | custom-call | tf_op jit(solution)/shard_map/pallas_call | solution.py:139
  166.8 1.5 slice.24
  168.3 0.3 reshape.485
  168.6 0.2 convert_multiply_fusion
  168.8 0.1 rev.17
  168.9 4.0 %fusion.40 = f32[16,4,5248]{2,0,1:T(8,128)S(1)} fusion(f32[16,4,5248]{2,0,1:T(8,128)S(1)} %rev.17), kind=kOutput, calls=%fused_computation.104 | output fusion | flops 1007616 | bytes 2686976 | tf_op jit(solution)/shard_map/jit(cumsum)/reduce_window_sum | solution.py:199
  172.9 0.7 slice.25
  173.7 26.6 %shard_map.77 = bf16[16,16,5248]{2,1,0:T(8,128)(2,1)} custom-call(s32[16]{0:T(128)} %copy-done.1, s32[16]{0:T(128)} %get-tuple-element.32.rowmap_ref, f32[16,32,1280]{2,1,0:T(8,128)} %bitcast.26, f32[16,80,1280]{2,1,0:T(8,128)} %sine_dynamic-update-slice_fusion.1.ph_ref), custom_call_target="tpu_custom_call" | custom-call | tf_op jit(solution)/shard_map/pallas_call | solution.py:139
  200.3 1.5 multiply_reduce_fusion
  201.8 0.1 add_convert_fusion
  202.0 1.1 copy.39
  (25 shorter events, 0.2 us)
Async XLA Ops:
  7.2 2.0 copy-start.2
  9.2 0.7 copy-start.5
  54.0 12.3 %copy-start.3 = (s32[512]{0:T(512)S(1)}, s32[512]{0:T(512)}, u32[]{:S(2)}) copy-start(s32[512]{0:T(512)} %param.9) | copy-start | bytes 6148
  54.0 13.5 %copy-start.4 = (f32[16]{0:T(128)S(1)}, f32[16]{0:T(128)}, u32[]{:S(2)}) copy-start(f32[16]{0:T(128)} %param.10) | copy-start | bytes 196
  54.0 86.1 %all-to-all-start = ((f32[64,20,512]{2,1,0:T(8,128)}), f32[64,20,512]{2,1,0:T(8,128)S(1)}, u32[]{:S(2)}, u32[]{:S(2)}) async-start(f32[64,20,512]{2,1,0:T(8,128)} %copy.34), calls=%async_computation | async-start | bytes 6291456 | tf_op jit(solution)/shard_map/all_to_all | solution.py:169
  66.3 134.0 %all-gather.3.cloned.1.call-start = ((), (), s32[]{:S(2)}) async-start(), calls=%async_computation.1 | async-start | bytes 1679360 | tf_op jit(solution)/shard_map/all_gather | solution.py:200
  67.0 32.5 %copy-start.1 = (s32[16]{0:T(128)}, s32[16]{0:T(128)S(1)}, u32[]{:S(2)}) copy-start(s32[16]{0:T(128)S(1)} %get-tuple-element.9.lengths_ref) | copy-start | bytes 196
  143.9 2.4 %copy-start = (f32[512,1280]{1,0:T(8,128)}, f32[512,1280]{1,0:T(8,128)S(1)}, u32[]{:S(2)}) copy-start(f32[512,1280]{1,0:T(8,128)S(1)} %copy.35) | copy-start | bytes 7864324
Sparse Core Ops, SparseCore 0:
  173.8 22.7 all-gather.2
where the time goes:
time: 211 us; the launch traced here: 210 us
  other arithmetic  48.2 us (23%)
  local copies, waits for them, and re-layouts  42.4 us (20%)
  Pallas kernels  42.4 us (20%)
  waiting for transfers between devices  40.5 us (19%)
  between operations  14.3 us (7%)
  starting transfers between devices  12.3 us (6%)
  matrix products  9.81 us (5%)
    pallas_call x2, Pallas kernels, synth(): pl.pallas_call(kernel, grid_spec=grid_spec, out_shape=jax.ShapeDtypeStruc...  42.4 us
    all_to_all x1, waiting for transfers between devices, local(): got = lax.all_to_all(send, 'wave', 0, 0, tiled=True)  40.5 us
    unnamed x7, other arithmetic  28.5 us
    all_to_all x1, starting transfers between devices, local(): got = lax.all_to_all(send, 'wave', 0, 0, tiled=True)  12.2 us
    dot_general x1, matrix products, local(): jnp.einsum('qaehci,qeit->qahct', lhs, legendre, preferred_element_type=jn...  9.81 us
    transpose x1, local copies, waits for them, and re-layouts, local(): bands.transpose(3, 0, 1, 4, 2)  9.46 us
    transpose x1, other arithmetic, local(): bands.transpose(3, 0, 1, 4, 2)  9.11 us
    reshape x1, local copies, waits for them, and re-layouts, local(): bands.transpose(3, 0, 1, 4, 2)  5.86 us
  transfers between devices with their start and end apart: 2, of which 1 were waited for; matrix products, arithmetic and copies ran while one was open for 16% of the time, Pallas kernels for 13%

commit v1 on v0

--- a/solution.py
+++ b/solution.py
@@ -160,13 +160,20 @@
     selected = coef[:, :, None, :, :] * selection[:, :, :, None, :]
     signs = jnp.array([[1.0, 1.0], [1.0, -1.0]], jnp.bfloat16)
     lhs = signs[None, :, :, None, None, None] * selected[:, None]
-    sums = jnp.einsum("qaehci,qeit->qahct", lhs, legendre, preferred_element_type=jnp.float32)
-    sums = sums.reshape(pair_local, 2, 2, cols, half_bands, band_rows)
-    north = sums[:, 0]
-    south = jnp.flip(sums[:, 1], 3)
-    bands = jnp.concatenate([north, south], 3)
-    send = bands.transpose(3, 0, 1, 4, 2).reshape(wave_count, pair_local * 2, band_rows * cols)
-    got = lax.all_to_all(send, "wave", 0, 0, tiled=True)
+    chunks = 2
+    part = pair_local // chunks
+    pieces = []
+    for k in range(chunks):
+        pick = slice(part * k, part * (k + 1))
+        sums = jnp.einsum("qaehci,qeit->qahct", lhs[pick], legendre[pick],
+                          preferred_element_type=jnp.float32)
+        sums = sums.reshape(part, 2, 2, cols, half_bands, band_rows)
+        north = sums[:, 0]
+        south = jnp.flip(sums[:, 1], 3)
+        bands = jnp.concatenate([north, south], 3)
+        send = bands.transpose(3, 0, 1, 4, 2).reshape(wave_count, part * 2, band_rows * cols)
+        pieces.append(lax.all_to_all(send, "wave", 0, 0, tiled=True))
+    got = jnp.concatenate(pieces, axis=1)
     slots = got.shape[0] * got.shape[1]
     fourier = got.reshape(slots, band_rows * cols).T.reshape(band_rows, cols, slots)
     south_side = (wave_rank >= half_bands).astype(jnp.int32)

time: 211 us -> 239 us (1.13)
  matrix products: 9.81 us -> 20.6 us
  starting transfers between devices: 12.3 us -> 23 us
  local copies, waits for them, and re-layouts: 42.4 us -> 45.2 us
  other arithmetic: 48.2 us -> 50.9 us
    dot_general x1 -> x2, matrix products: 9.81 us -> 20.6 us  [local(): jnp.einsum('qaehci,qeit->qahct', lhs[pick], legendre[pick], preferred_ele...]
    all_to_all x1 -> x2, starting transfers between devices: 12.2 us -> 23 us  [local(): pieces.append(lax.all_to_all(send, 'wave', 0, 0, tiled=True))]
    concatenate x0 -> x1, other arithmetic: none -> 2.77 us  [local(): got = jnp.concatenate(pieces, axis=1)]
    squeeze x1 -> x2, local copies, waits for them, and re-layouts: 4.69 us -> 6.51 us  [local(): north = sums[:, 0]]
    rev x1 -> x2, local copies, waits for them, and re-layouts: 5.24 us -> 7.02 us  [local(): south = jnp.flip(sums[:, 1], 3)]
    transpose x1 -> x2, local copies, waits for them, and re-layouts: 9.46 us -> 8.85 us  [local(): bands.transpose(3, 0, 1, 4, 2)]
    all_to_all x1 -> x2, waiting for transfers between devices: 40.5 us -> 41 us  [local(): pieces.append(lax.all_to_all(send, 'wave', 0, 0, tiled=True))]
    reshape x1 -> x2, local copies, waits for them, and re-layouts: 5.86 us -> 5.67 us  [local(): bands.transpose(3, 0, 1, 4, 2)]
  transfers between devices with their start and end apart: 2 -> 3, of which waited for: 1 -> 1; matrix products, arithmetic and copies ran while one was open for 16% -> 27% of each run, Pallas kernels for 13% -> 11%
where the time goes in v1:
time: 239 us; the launch traced here: 238 us
  other arithmetic  50.9 us (21%)
  local copies, waits for them, and re-layouts  45.2 us (19%)
  Pallas kernels  42.6 us (18%)
  waiting for transfers between devices  41 us (17%)
  starting transfers between devices  23 us (10%)
  matrix products  20.6 us (9%)
  between operations  14.3 us (6%)
    pallas_call x2, Pallas kernels, synth(): pl.pallas_call(kernel, grid_spec=grid_spec, out_shape=jax.ShapeDtypeStruc...  42.6 us
    all_to_all x2, waiting for transfers between devices, local(): pieces.append(lax.all_to_all(send, 'wave', 0, 0, tiled=True))  41 us
    unnamed x7, other arithmetic  28.3 us
    all_to_all x2, starting transfers between devices, local(): pieces.append(lax.all_to_all(send, 'wave', 0, 0, tiled=True))  23 us
    dot_general x2, matrix products, local(): jnp.einsum('qaehci,qeit->qahct', lhs[pick], legendre[pick], preferred_ele...  20.6 us
    transpose x2, other arithmetic, local(): bands.transpose(3, 0, 1, 4, 2)  9.15 us
    transpose x2, local copies, waits for them, and re-layouts, local(): bands.transpose(3, 0, 1, 4, 2)  8.85 us
    rev x2, local copies, waits for them, and re-layouts, local(): south = jnp.flip(sums[:, 1], 3)  7.02 us
  transfers between devices with their start and end apart: 3, of which 1 were waited for; matrix products, arithmetic and copies ran while one was open for 27% of the time, Pallas kernels for 11%

profile of v1, /device:TPU:2, one launch (start us, length us, event | category | flops | bytes accessed | tf_op | source)
XLA Modules:
  0.0 237.8 jit_solution(9079979742681984438)
XLA Ops:
  7.2 1.9 copy.36
  9.1 0.1 copy.37
  9.4 0.1 iota_compare_fusion.1
  9.6 0.2 broadcast_multiply_fusion
  9.8 10.0 %fusion = f32[5,2,2,32,512,1]{3,4,5,2,1,0:T(8,128)S(1)} fusion(bf16[10,2,640,512]{3,2,1,0:T(8,128)(2,1)} %param.7, bf16[10,2,2,32,640]{4,3,1,2,0:T(8,128)(2,1)S(1)} %broadcast_multiply_fusion, bf16[2,2]{1,0:T(2,128)(2,1)S(1)} %copy-done.7), kind=kOutput, calls=%fused_computation | convolution fusion | flops 845414400 | bytes 9502728 | tf_op jit(solution)/shard_map/qaehci,qeit->qahct/dot_general | solution.py:168
  19.8 2.0 slice_bitcast_fusion.1
  21.8 3.5 %rev.20 = f32[5,2,32,32,16]{2,4,3,1,0:T(8,128)} reverse(f32[5,2,32,32,16]{2,4,3,1,0:T(8,128)} %get-tuple-element.15), dimensions={3} | reverse | bytes 1310720 | tf_op jit(solution)/shard_map/jit(_flip)/rev | solution.py:172
  25.3 4.6 %maximum_bitcast_fusion.1 = f32[64,5,2,16,32]{4,3,0,2,1:T(8,128)} fusion(f32[5,2,32,32,16]{2,4,3,1,0:T(8,128)} %rev.20, f32[5,2,32,32,16]{2,4,3,1,0:T(8,128)S(1)} %get-tuple-element.14), kind=kLoop, calls=%fused_computation.7 | loop fusion | flops 327680 | bytes 2621440 | tf_op jit(solution)/shard_map/transpose | solution.py:174
  29.9 4.4 %copy.44 = f32[64,5,2,16,32]{0,4,3,2,1:T(8,128)S(1)} copy(f32[64,5,2,16,32]{4,3,0,2,1:T(8,128)} %maximum_bitcast_fusion.1) | data formatting | bytes 2621440 | tf_op jit(solution)/shard_map/transpose | solution.py:174
  34.3 2.8 %copy.45 = f32[64,10,512]{2,1,0:T(8,128)} copy(f32[64,10,512]{0,2,1:T(8,128)S(1)} %bitcast.45) | data formatting | bytes 2621440 | tf_op jit(solution)/shard_map/reshape | solution.py:174
  37.2 12.7 %all-to-all-start.1 = ((f32[64,10,512]{2,1,0:T(8,128)}), f32[64,10,512]{2,1,0:T(8,128)}, u32[]{:S(2)}, u32[]{:S(2)}) async-start(f32[64,10,512]{2,1,0:T(8,128)} %copy.45), calls=%async_computation.1 | async-start | bytes 4194304 | tf_op jit(solution)/shard_map/all_to_all | solution.py:175
  49.9 10.7 %fusion.2 = f32[5,2,2,32,512,1]{3,4,5,2,1,0:T(8,128)} fusion(bf16[10,2,640,512]{3,2,1,0:T(8,128)(2,1)} %param.7, bf16[10,2,2,32,640]{4,3,1,2,0:T(8,128)(2,1)S(1)} %copy-done.2, bf16[2,2]{1,0:T(2,128)(2,1)S(1)} %copy-done.7), kind=kOutput, calls=%fused_computation.2 | convolution fusion | flops 845414400 | bytes 9502728 | tf_op jit(solution)/shard_map/qaehci,qeit->qahct/dot_general | solution.py:168
  60.6 0.1 rev.18
  60.7 4.5 %slice_bitcast_fusion.3 = (f32[5,2,32,32,16]{2,4,3,1,0:T(8,128)S(1)}, f32[5,2,32,32,16]{2,4,3,1,0:T(8,128)}) fusion(f32[5,2,2,32,32,16]{3,5,4,2,1,0:T(8,128)} %bitcast.47), kind=kLoop, calls=%fused_computation.16 | loop fusion | bytes 2621440 | tf_op jit(solution)/shard_map/squeeze | solution.py:171
  65.2 3.5 %rev.19 = f32[5,2,32,32,16]{2,4,3,1,0:T(8,128)} reverse(f32[5,2,32,32,16]{2,4,3,1,0:T(8,128)} %get-tuple-element.13), dimensions={3} | reverse | bytes 1310720 | tf_op jit(solution)/shard_map/jit(_flip)/rev | solution.py:172
  68.7 0.2 copy.47
  68.9 0.2 mul.254
  69.1 0.6 fusion.46
  69.8 4.6 %maximum_bitcast_fusion = f32[64,5,2,16,32]{4,3,0,2,1:T(8,128)} fusion(f32[5,2,32,32,16]{2,4,3,1,0:T(8,128)} %rev.19, f32[5,2,32,32,16]{2,4,3,1,0:T(8,128)S(1)} %get-tuple-element.12), kind=kLoop, calls=%fused_computation.6 | loop fusion | flops 327680 | bytes 2621440 | tf_op jit(solution)/shard_map/transpose | solution.py:174
  74.5 4.4 %copy.40 = f32[64,5,2,16,32]{0,4,3,2,1:T(8,128)S(1)} copy(f32[64,5,2,16,32]{4,3,0,2,1:T(8,128)} %maximum_bitcast_fusion) | data formatting | bytes 2621440 | tf_op jit(solution)/shard_map/transpose | solution.py:174
  79.0 2.8 %copy.41 = f32[64,10,512]{2,1,0:T(8,128)} copy(f32[64,10,512]{0,2,1:T(8,128)S(1)} %bitcast.46) | data formatting | bytes 2621440 | tf_op jit(solution)/shard_map/reshape | solution.py:174
  81.9 5.9 %cosine_dynamic-update-slice_fusion = f32[16,80,1280]{2,1,0:T(8,128)} fusion(f32[16]{0:T(128)S(1)} %broadcast_divide_fusion, s32[16]{0:T(128)S(1)} %get-tuple-element.9.lengths_ref, f32[16]{0:T(128)S(1)} %convert_element_type.103, f32[16,1280]{1,0:T(8,128)S(1)} %get-tuple-element.27, s32[16,1280]{1,0:T(8,128)S(1)} %get-tuple-element.26), kind=kLoop, calls=%fused_computation.39 | loop fusion | flops 4259839 | bytes 1474752
  87.7 5.9 %sine_dynamic-update-slice_fusion = f32[16,80,1280]{2,1,0:T(8,128)} fusion(f32[16,80,1280]{2,1,0:T(8,128)} %cosine_dynamic-update-slice_fusion, f32[16]{0:T(128)S(1)} %broadcast_divide_fusion, s32[16]{0:T(128)S(1)} %get-tuple-element.9.lengths_ref, f32[16]{0:T(128)S(1)} %convert_element_type.103, f32[16,1280]{1,0:T(8,128)S(1)} %get-tuple-element.27, ...), kind=kLoop, calls=%fused_computation.38 | loop fusion | flops 4259840 | bytes 1474752
  93.6 3.3 %cosine_dynamic-update-slice_fusion.2 = f32[16,80,1280]{2,1,0:T(8,128)} fusion(f32[16,80,1280]{2,1,0:T(8,128)} %sine_dynamic-update-slice_fusion, f32[16]{0:T(128)S(1)} %broadcast_divide_fusion, s32[16]{0:T(128)S(1)} %get-tuple-element.9.lengths_ref, f32[16]{0:T(128)S(1)} %convert_element_type.103, f32[8,1280]{1,0:T(8,128)S(1)} %get-tuple-element.24, ...), kind=kLoop, calls=%fused_computation.65 | loop fusion | flops 2129920 | bytes 737472
  96.9 3.3 %sine_dynamic-update-slice_fusion.2 = f32[16,80,1280]{2,1,0:T(8,128)} fusion(f32[16,80,1280]{2,1,0:T(8,128)} %cosine_dynamic-update-slice_fusion.2, f32[16]{0:T(128)S(1)} %broadcast_divide_fusion, s32[16]{0:T(128)S(1)} %get-tuple-element.9.lengths_ref, f32[16]{0:T(128)S(1)} %convert_element_type.103, f32[8,1280]{1,0:T(8,128)S(1)} %get-tuple-element.24, ...), kind=kLoop, calls=%fused_computation.64 | loop fusion | flops 2129920 | bytes 737472
  100.2 3.3 %multiply_dynamic-update-slice_fusion.1 = f32[16,80,1280]{2,1,0:T(8,128)} fusion(f32[16,80,1280]{2,1,0:T(8,128)} %sine_dynamic-update-slice_fusion.2, f32[16,1280]{1,0:T(8,128)S(1)} %compare_convert_fusion, f32[16]{0:T(128)S(1)} %broadcast_divide_fusion, s32[16]{0:T(128)S(1)} %get-tuple-element.9.lengths_ref, f32[16]{0:T(128)S(1)} %convert_element_type.103, ...), kind=kLoop, calls=%fused_computation.63 | loop fusion | flops 2293760 | bytes 819392
  103.5 10.3 %all-to-all-start = ((f32[64,10,512]{2,1,0:T(8,128)}), f32[64,10,512]{2,1,0:T(8,128)}, u32[]{:S(2)}, u32[]{:S(2)}) async-start(f32[64,10,512]{2,1,0:T(8,128)} %copy.41), calls=%async_computation | async-start | bytes 4194304 | tf_op jit(solution)/shard_map/all_to_all | solution.py:175
  113.9 3.4 %multiply_dynamic-update-slice_fusion = f32[16,80,1280]{2,1,0:T(8,128)} fusion(f32[16,80,1280]{2,1,0:T(8,128)} %multiply_dynamic-update-slice_fusion.1, f32[16,1280]{1,0:T(8,128)S(1)} %compare_convert_fusion, f32[16]{0:T(128)S(1)} %broadcast_divide_fusion, s32[16]{0:T(128)S(1)} %get-tuple-element.9.lengths_ref, f32[16]{0:T(128)S(1)} %convert_element_type.103, ...), kind=kLoop, calls=%fused_computation.62 | loop fusion | flops 2293760 | bytes 819392
  117.2 3.3 %cosine_dynamic-update-slice_fusion.1 = f32[16,80,1280]{2,1,0:T(8,128)} fusion(f32[16,80,1280]{2,1,0:T(8,128)} %multiply_dynamic-update-slice_fusion, f32[16]{0:T(128)S(1)} %broadcast_divide_fusion, s32[16]{0:T(128)S(1)} %get-tuple-element.9.lengths_ref, f32[16]{0:T(128)S(1)} %convert_element_type.103, f32[8,1280]{1,0:T(8,128)S(1)} %get-tuple-element.17, ...), kind=kLoop, calls=%fused_computation.61 | loop fusion | flops 2129920 | bytes 737472
  120.6 3.3 %sine_dynamic-update-slice_fusion.1.ph_ref = f32[16,80,1280]{2,1,0:T(8,128)} fusion(f32[16,80,1280]{2,1,0:T(8,128)} %cosine_dynamic-update-slice_fusion.1, f32[16]{0:T(128)S(1)} %broadcast_divide_fusion, s32[16]{0:T(128)S(1)} %get-tuple-element.9.lengths_ref, f32[16]{0:T(128)S(1)} %convert_element_type.103, f32[8,1280]{1,0:T(8,128)S(1)} %get-tuple-element.17, ...), kind=kLoop, calls=%fused_computation.60 | loop fusion | flops 2129920 | bytes 737472 | tf_op jit(solution)/shard_map/concatenate | solution.py:57
  123.9 0.1 iota_compare_fusion
  124.0 41.0 %all-to-all-done = f32[64,10,512]{2,1,0:T(8,128)} async-done(((f32[64,10,512]{2,1,0:T(8,128)}), f32[64,10,512]{2,1,0:T(8,128)}, u32[]{:S(2)}, u32[]{:S(2)}) %all-to-all-start) | async-done | bytes 1310752 | tf_op jit(solution)/shard_map/all_to_all | solution.py:175
  165.0 2.8 %pad_maximum_fusion = f32[64,20,512]{2,1,0:T(8,128)S(1)} fusion(f32[64,10,512]{2,1,0:T(8,128)} %all-to-all-done.1, f32[64,10,512]{2,1,0:T(8,128)} %all-to-all-done), kind=kLoop, calls=%fused_computation.12 | loop fusion | flops 655360 | bytes 5242880 | tf_op jit(solution)/shard_map/concatenate | solution.py:176
  167.8 1.6 reshape.485
  169.4 2.1 copy.46
  171.6 2.3 reshape_reshape.3
  173.9 3.6 %slice_reduce_fusion = f32[16,2,4,1280]{3,2,1,0:T(4,128)S(1)} fusion(f32[16,2,4,4,1280]{4,3,2,1,0:T(4,128)} %reshape_reshape.3), kind=kLoop, calls=%fused_computation.59 | loop fusion | bytes 1310720 | tf_op jit(solution)/shard_map/slice | solution.py:187
  177.5 1.1 reshape_squeeze.3.f_ref
  178.6 15.8 %shard_map.78 = f32[16,192,128]{2,1,0:T(8,128)} custom-call(s32[16]{0:T(128)} %copy-done.3, s32[16]{0:T(128)} %get-tuple-element.34.rowmap_ref, f32[16,8,1280]{2,1,0:T(8,128)} %reshape_squeeze.3.f_ref, f32[16,80,1280]{2,1,0:T(8,128)} %sine_dynamic-update-slice_fusion.1.ph_ref), custom_call_target="tpu_custom_call" | custom-call | tf_op jit(solution)/shard_map/pallas_call | solution.py:139
  194.4 1.5 slice.50
  196.0 0.3 reshape.495
  196.3 0.2 convert_multiply_fusion
  196.6 4.0 %fusion.47 = f32[16,4,5248]{2,0,1:T(8,128)S(1)} fusion(f32[16,4,5248]{2,0,1:T(8,128)S(1)} %rev.21), kind=kOutput, calls=%fused_computation.115 | output fusion | flops 1007616 | bytes 2686976 | tf_op jit(solution)/shard_map/jit(cumsum)/reduce_window_sum | solution.py:206
  200.6 0.7 slice.51
  201.4 26.8 %shard_map.77 = bf16[16,16,5248]{2,1,0:T(8,128)(2,1)} custom-call(s32[16]{0:T(128)} %copy-done.3, s32[16]{0:T(128)} %get-tuple-element.34.rowmap_ref, f32[16,32,1280]{2,1,0:T(8,128)} %bitcast.43, f32[16,80,1280]{2,1,0:T(8,128)} %sine_dynamic-update-slice_fusion.1.ph_ref), custom_call_target="tpu_custom_call" | custom-call | tf_op jit(solution)/shard_map/pallas_call | solution.py:139
  228.2 1.5 multiply_reduce_fusion
  229.7 0.1 add_convert_fusion
  229.8 1.1 copy.50
  (38 shorter events, 0.7 us)
Async XLA Ops:
  7.2 2.0 copy-start.4
  7.2 2.6 %copy-start.7 = (bf16[2,2]{1,0:T(2,128)(2,1)S(1)}, bf16[2,2]{1,0:T(2,128)(2,1)}, u32[]{:S(2)}) copy-start(bf16[2,2]{1,0:T(2,128)(2,1)} %constant.78.clone) | copy-start | bytes 28
  9.8 10.0 %copy-start.1 = (bf16[10,2,2,32,640]{4,3,1,2,0:T(8,128)(2,1)}, bf16[10,2,2,32,640]{4,3,1,2,0:T(8,128)(2,1)S(1)}, u32[]{:S(2)}) copy-start(bf16[10,2,2,32,640]{4,3,1,2,0:T(8,128)(2,1)S(1)} %broadcast_multiply_fusion) | copy-start | bytes 4915204
  37.2 12.7 %copy-start.2 = (bf16[10,2,2,32,640]{4,3,1,2,0:T(8,128)(2,1)S(1)}, bf16[10,2,2,32,640]{4,3,1,2,0:T(8,128)(2,1)}, u32[]{:S(2)}) copy-start(bf16[10,2,2,32,640]{4,3,1,2,0:T(8,128)(2,1)} %copy-done.1) | copy-start | bytes 4915204
  37.2 66.3 %all-to-all-start.1 = ((f32[64,10,512]{2,1,0:T(8,128)}), f32[64,10,512]{2,1,0:T(8,128)}, u32[]{:S(2)}, u32[]{:S(2)}) async-start(f32[64,10,512]{2,1,0:T(8,128)} %copy.45), calls=%async_computation.1 | async-start | bytes 4194304 | tf_op jit(solution)/shard_map/all_to_all | solution.py:175
  49.8 10.7 %copy-start.5 = (s32[512]{0:T(512)S(1)}, s32[512]{0:T(512)}, u32[]{:S(2)}) copy-start(s32[512]{0:T(512)} %param.9) | copy-start | bytes 6148
  69.7 54.2 %copy-start.3 = (s32[16]{0:T(128)}, s32[16]{0:T(128)S(1)}, u32[]{:S(2)}) copy-start(s32[16]{0:T(128)S(1)} %get-tuple-element.9.lengths_ref) | copy-start | bytes 196
  78.9 2.8 %copy-start.6 = (f32[16]{0:T(128)S(1)}, f32[16]{0:T(128)}, u32[]{:S(2)}) copy-start(f32[16]{0:T(128)} %param.10) | copy-start | bytes 196
  103.5 61.5 %all-to-all-start = ((f32[64,10,512]{2,1,0:T(8,128)}), f32[64,10,512]{2,1,0:T(8,128)}, u32[]{:S(2)}, u32[]{:S(2)}) async-start(f32[64,10,512]{2,1,0:T(8,128)} %copy.41), calls=%async_computation | async-start | bytes 4194304 | tf_op jit(solution)/shard_map/all_to_all | solution.py:175
  113.8 114.4 %all-gather.3.cloned.1.call-start = ((), (), s32[]{:S(2)}) async-start(), calls=%async_computation.2 | async-start | bytes 1679360 | tf_op jit(solution)/shard_map/all_gather | solution.py:207
  171.6 2.4 copy-start
Sparse Core Ops, SparseCore 0:
  201.5 22.8 all-gather.2

commit v2 on v0

--- a/solution.py
+++ b/solution.py
@@ -177,18 +177,9 @@
     points_all = jnp.concatenate([row_points, jnp.flip(row_points)])
     lengths = lax.dynamic_slice_in_dim(points_all, wave_rank * band_rows, band_rows)
     ph = tables(wave_numbers, lengths)
-    heat_cols = fourier.reshape(band_rows, 2, fields // QUANTITY_COUNT, QUANTITY_COUNT, slots)[:, :, :, 0]
-    heat_cols = heat_cols.reshape(band_rows, 2 * fields // QUANTITY_COUNT, slots)
-    heat_fields = fields // QUANTITY_COUNT
-    depth = DEPTH
-    raw = synth(heat_kernel, heat_cols, ph, lengths, rowmap,
-                heat_fields * depth, BLOCK, jnp.float32, heat_fields * depth)
-    raw = raw.reshape(band_rows, heat_fields, depth, BLOCK)[:, :, :BLOCKS].reshape(band_rows, heat_fields, LCAP)
-    position = jnp.arange(LCAP, dtype=jnp.int32)
-    raw = jnp.where(position[None, None, :] < lengths[:, None, None], raw, 0.0)
-    heat_state_values = raw.astype(jnp.bfloat16).astype(jnp.float32)
     values = synth(main_kernel, fourier, ph, lengths, rowmap,
                    fields, LCAP, jnp.bfloat16, fields * BLOCKS)
+    heat_state_values = values[:, 0::QUANTITY_COUNT, :].astype(jnp.float32)
 
     device_layers = heat_state_values.shape[1]
     lev_rank = lax.axis_index("lev")
@@ -197,10 +188,12 @@
     )
     scaled_heat_values = heat_state_values * layer_depth_factor[None, :, None]
     partial_totals = jnp.flip(jnp.cumsum(jnp.flip(scaled_heat_values, 1), axis=1), 1)
-    everything = lax.all_gather(partial_totals[:, 0, :], "lev")
-    lev_count = everything.shape[0]
-    below = (jnp.arange(lev_count) > lev_rank).astype(jnp.float32)[:, None, None]
-    deeper = jnp.sum(everything * below, axis=0)
+    lev_count = lax.axis_size("lev")
+    bottom = partial_totals[:, 0, :]
+    next_one = lax.ppermute(bottom, "lev", [(d + 1, d) for d in range(lev_count - 1)])
+    pair_sum = bottom + next_one
+    next_two = lax.ppermute(pair_sum, "lev", [(d + 2, d) for d in range(lev_count - 2)])
+    deeper = next_one + next_two
     geopotential = (partial_totals + deeper[:, None, :]).astype(jnp.bfloat16)
     return (values, geopotential)
 

time: 211 us -> 206 us (0.976)
  Pallas kernels: 42.4 us -> 27 us
  waiting for transfers between devices: 40.5 us -> 55.6 us
  between operations: 14.3 us -> 0.88 us
  local copies, waits for them, and re-layouts: 42.4 us -> 46.7 us
  starting transfers between devices: 12.3 us -> 15.9 us
    pallas_call x2 -> x1, Pallas kernels: 42.4 us -> 27 us  [synth(): pl.pallas_call(kernel, grid_spec=grid_spec, out_shape=jax.ShapeDtypeStruc...]
    ppermute x0 -> x2, waiting for transfers between devices: none -> 15 us  [the longest x1 7.86 us: local(): lax.ppermute(bottom, 'lev', [(d + 1, d) for d in range(lev_count - 1)])]
    ppermute x0 -> x2, starting transfers between devices: none -> 3.49 us  [the longest x1 2.21 us: local(): lax.ppermute(bottom, 'lev', [(d + 1, d) for d in range(lev_count - 1)])]
    another operation x2 -> x0, local copies, waits for them, and re-layouts: 3.4 us -> none  [the longest x1 2.34 us: local(): fourier.reshape(band_rows, 2, fields // QUANTITY_COUNT, QUANTITY_COUNT, s...]
    slice x3 -> x2, local copies, waits for them, and re-layouts: 5.88 us -> 9.03 us  [the longest x1 8.69 us: local(): heat_state_values = values[:, 0::QUANTITY_COUNT, :].astype(jnp.float32)]
    rev x0 -> x1, local copies, waits for them, and re-layouts: none -> 2.45 us  [local(): jnp.flip(jnp.cumsum(jnp.flip(scaled_heat_values, 1), axis=1), 1)]
    rev x1, local copies, waits for them, and re-layouts: 0.09 us -> 2.45 us  [local(): jnp.flip(scaled_heat_values, 1)]
  transfers between devices with their start and end apart: 2 -> 3, of which waited for: 1 -> 3; matrix products, arithmetic and copies ran while one was open for 16% -> 17% of each run, Pallas kernels for 13% -> 0%
where the time goes in v2:
time: 206 us; the launch traced here: 204 us
  waiting for transfers between devices  55.6 us (27%)
  other arithmetic  47.9 us (23%)
  local copies, waits for them, and re-layouts  46.7 us (23%)
  Pallas kernels  27 us (13%)
  starting transfers between devices  15.9 us (8%)
  matrix products  9.83 us (5%)
    all_to_all x1, waiting for transfers between devices, local(): got = lax.all_to_all(send, 'wave', 0, 0, tiled=True)  40.6 us
    unnamed x7, other arithmetic  28.4 us
    pallas_call x1, Pallas kernels, synth(): pl.pallas_call(kernel, grid_spec=grid_spec, out_shape=jax.ShapeDtypeStruc...  27 us
    all_to_all x1, starting transfers between devices, local(): got = lax.all_to_all(send, 'wave', 0, 0, tiled=True)  12.4 us
    dot_general x1, matrix products, local(): jnp.einsum('qaehci,qeit->qahct', lhs, legendre, preferred_element_type=jn...  9.83 us
    transpose x1, local copies, waits for them, and re-layouts, local(): bands.transpose(3, 0, 1, 4, 2)  9.47 us
    transpose x1, other arithmetic, local(): bands.transpose(3, 0, 1, 4, 2)  9.12 us
    slice x1, local copies, waits for them, and re-layouts, local(): heat_state_values = values[:, 0::QUANTITY_COUNT, :].astype(jnp.float32)  8.69 us
  transfers between devices with their start and end apart: 3, of which 3 were waited for; matrix products, arithmetic and copies ran while one was open for 17% of the time, Pallas kernels for 0%

profile of v2, /device:TPU:2, one launch (start us, length us, event | category | flops | bytes accessed | tf_op | source)
XLA Modules:
  0.0 203.8 jit_solution(12698991720705062797)
XLA Ops:
  0.6 0.0 copy-start.1
  0.6 0.0 copy-start.4
  0.7 1.9 copy.23
  2.5 0.1 copy.24
  2.7 0.1 broadcast_subtract_fusion.1
  2.8 0.1 fusion.30
  2.8 0.1 iota_compare_fusion
  3.0 0.1 add_convert_fusion.1
  3.1 0.2 broadcast_multiply_fusion
  3.3 9.8 %fusion = f32[10,2,2,32,512,1]{3,4,5,2,1,0:T(8,128)S(1)} fusion(bf16[10,2,640,512]{3,2,1,0:T(8,128)(2,1)} %param.7, bf16[10,2,2,32,640]{4,3,1,2,0:T(8,128)(2,1)S(1)} %broadcast_multiply_fusion, bf16[2,2]{1,0:T(2,128)(2,1)S(1)} %copy-done.4), kind=kOutput, calls=%fused_computation | convolution fusion | flops 1679360000 | bytes 17367048 | tf_op jit(solution)/shard_map/qaehci,qeit->qahct/dot_general | solution.py:163
  13.1 4.7 %slice_bitcast_fusion.1 = (f32[10,2,32,32,16]{2,4,3,1,0:T(8,128)}, f32[10,2,32,32,16]{2,4,3,1,0:T(8,128)}) fusion(f32[10,2,2,32,32,16]{3,5,4,2,1,0:T(8,128)S(1)} %bitcast.29), kind=kLoop, calls=%fused_computation.4 | loop fusion | bytes 5242880 | tf_op jit(solution)/shard_map/squeeze | solution.py:165
  17.8 5.2 %rev.16 = f32[10,2,32,32,16]{2,4,3,1,0:T(8,128)} reverse(f32[10,2,32,32,16]{2,4,3,1,0:T(8,128)} %get-tuple-element.7), dimensions={3} | reverse | bytes 2621440 | tf_op jit(solution)/shard_map/jit(_flip)/rev | solution.py:166
  23.1 9.1 %maximum_bitcast_fusion = f32[64,10,2,16,32]{4,3,0,2,1:T(8,128)} fusion(f32[10,2,32,32,16]{2,4,3,1,0:T(8,128)} %rev.16, f32[10,2,32,32,16]{2,4,3,1,0:T(8,128)} %get-tuple-element.6), kind=kLoop, calls=%fused_computation.2 | loop fusion | flops 655360 | bytes 5242880 | tf_op jit(solution)/shard_map/transpose | solution.py:168
  32.2 9.5 %copy.27 = f32[64,10,2,16,32]{0,4,3,2,1:T(8,128)} copy(f32[64,10,2,16,32]{4,3,0,2,1:T(8,128)} %maximum_bitcast_fusion) | data formatting | bytes 5242880 | tf_op jit(solution)/shard_map/transpose | solution.py:168
  41.7 5.8 %copy.28 = f32[64,20,512]{2,1,0:T(8,128)} copy(f32[64,20,512]{0,2,1:T(8,128)} %bitcast.28) | data formatting | bytes 5242880 | tf_op jit(solution)/shard_map/reshape | solution.py:168
  47.4 12.4 %all-to-all-start = ((f32[64,20,512]{2,1,0:T(8,128)}), f32[64,20,512]{2,1,0:T(8,128)S(1)}, u32[]{:S(2)}, u32[]{:S(2)}) async-start(f32[64,20,512]{2,1,0:T(8,128)} %copy.28), calls=%async_computation | async-start | bytes 6291456 | tf_op jit(solution)/shard_map/all_to_all | solution.py:169
  59.9 0.1 rev.15
  60.0 0.2 copy.30
  60.2 0.2 mul.246
  60.4 0.5 fusion.38
  61.0 0.1 compare_convert_fusion
  61.0 0.0 copy-done.3
  61.1 0.1 dynamic_slice.11
  61.2 0.1 broadcast_multiply_fusion.1
  61.3 5.9 %cosine_dynamic-update-slice_fusion = f32[16,80,1280]{2,1,0:T(8,128)} fusion(f32[16]{0:T(128)S(1)} %broadcast_divide_fusion, s32[16]{0:T(128)S(1)} %get-tuple-element.3.lengths_ref, f32[16]{0:T(128)S(1)} %convert_element_type.93, f32[16,1280]{1,0:T(8,128)S(1)} %get-tuple-element.19, s32[16,1280]{1,0:T(8,128)S(1)} %get-tuple-element.18), kind=kLoop, calls=%fused_computation.25 | loop fusion | flops 4259839 | bytes 1474752
  67.2 5.9 %sine_dynamic-update-slice_fusion = f32[16,80,1280]{2,1,0:T(8,128)} fusion(f32[16,80,1280]{2,1,0:T(8,128)} %cosine_dynamic-update-slice_fusion, f32[16]{0:T(128)S(1)} %broadcast_divide_fusion, s32[16]{0:T(128)S(1)} %get-tuple-element.3.lengths_ref, f32[16]{0:T(128)S(1)} %convert_element_type.93, f32[16,1280]{1,0:T(8,128)S(1)} %get-tuple-element.19, ...), kind=kLoop, calls=%fused_computation.24 | loop fusion | flops 4259840 | bytes 1474752
  73.0 3.3 %cosine_dynamic-update-slice_fusion.2 = f32[16,80,1280]{2,1,0:T(8,128)} fusion(f32[16,80,1280]{2,1,0:T(8,128)} %sine_dynamic-update-slice_fusion, f32[16]{0:T(128)S(1)} %broadcast_divide_fusion, s32[16]{0:T(128)S(1)} %get-tuple-element.3.lengths_ref, f32[16]{0:T(128)S(1)} %convert_element_type.93, f32[8,1280]{1,0:T(8,128)S(1)} %get-tuple-element.16, ...), kind=kLoop, calls=%fused_computation.50 | loop fusion | flops 2129920 | bytes 737472
  76.3 3.3 %sine_dynamic-update-slice_fusion.2 = f32[16,80,1280]{2,1,0:T(8,128)} fusion(f32[16,80,1280]{2,1,0:T(8,128)} %cosine_dynamic-update-slice_fusion.2, f32[16]{0:T(128)S(1)} %broadcast_divide_fusion, s32[16]{0:T(128)S(1)} %get-tuple-element.3.lengths_ref, f32[16]{0:T(128)S(1)} %convert_element_type.93, f32[8,1280]{1,0:T(8,128)S(1)} %get-tuple-element.16, ...), kind=kLoop, calls=%fused_computation.49 | loop fusion | flops 2129920 | bytes 737472
  79.7 3.3 %multiply_dynamic-update-slice_fusion.1 = f32[16,80,1280]{2,1,0:T(8,128)} fusion(f32[16,80,1280]{2,1,0:T(8,128)} %sine_dynamic-update-slice_fusion.2, f32[16,1280]{1,0:T(8,128)S(1)} %compare_convert_fusion, f32[16]{0:T(128)S(1)} %broadcast_divide_fusion, s32[16]{0:T(128)S(1)} %get-tuple-element.3.lengths_ref, f32[16]{0:T(128)S(1)} %convert_element_type.93, ...), kind=kLoop, calls=%fused_computation.48 | loop fusion | flops 2293760 | bytes 819392
  83.0 3.3 %multiply_dynamic-update-slice_fusion = f32[16,80,1280]{2,1,0:T(8,128)} fusion(f32[16,80,1280]{2,1,0:T(8,128)} %multiply_dynamic-update-slice_fusion.1, f32[16,1280]{1,0:T(8,128)S(1)} %compare_convert_fusion, f32[16]{0:T(128)S(1)} %broadcast_divide_fusion, s32[16]{0:T(128)S(1)} %get-tuple-element.3.lengths_ref, f32[16]{0:T(128)S(1)} %convert_element_type.93, ...), kind=kLoop, calls=%fused_computation.47 | loop fusion | flops 2293760 | bytes 819392
  86.3 3.3 %cosine_dynamic-update-slice_fusion.1 = f32[16,80,1280]{2,1,0:T(8,128)} fusion(f32[16,80,1280]{2,1,0:T(8,128)} %multiply_dynamic-update-slice_fusion, f32[16]{0:T(128)S(1)} %broadcast_divide_fusion, s32[16]{0:T(128)S(1)} %get-tuple-element.3.lengths_ref, f32[16]{0:T(128)S(1)} %convert_element_type.93, f32[8,1280]{1,0:T(8,128)S(1)} %get-tuple-element.9, ...), kind=kLoop, calls=%fused_computation.46 | loop fusion | flops 2129920 | bytes 737472
  89.6 3.3 %sine_dynamic-update-slice_fusion.1.ph_ref = f32[16,80,1280]{2,1,0:T(8,128)} fusion(f32[16,80,1280]{2,1,0:T(8,128)} %cosine_dynamic-update-slice_fusion.1, f32[16]{0:T(128)S(1)} %broadcast_divide_fusion, s32[16]{0:T(128)S(1)} %get-tuple-element.3.lengths_ref, f32[16]{0:T(128)S(1)} %convert_element_type.93, f32[8,1280]{1,0:T(8,128)S(1)} %get-tuple-element.9, ...), kind=kLoop, calls=%fused_computation.45 | loop fusion | flops 2129920 | bytes 737472 | tf_op jit(solution)/shard_map/concatenate | solution.py:57
  93.0 40.6 %all-to-all-done = f32[64,20,512]{2,1,0:T(8,128)S(1)} async-done(((f32[64,20,512]{2,1,0:T(8,128)}), f32[64,20,512]{2,1,0:T(8,128)S(1)}, u32[]{:S(2)}, u32[]{:S(2)}) %all-to-all-start) | async-done | bytes 2621472 | tf_op jit(solution)/shard_map/all_to_all | solution.py:169
  133.6 1.6 reshape.448
  135.2 3.3 %copy.29 = f32[512,1280]{1,0:T(8,128)} copy(f32[512,1280]{0,1:T(8,128)} %bitcast.30) | data formatting | bytes 5242880 | tf_op jit(solution)/shard_map/transpose | solution.py:171
  138.5 27.0 %shard_map.77 = bf16[16,16,5248]{2,1,0:T(8,128)(2,1)} custom-call(s32[16]{0:T(128)} %copy-done, s32[16]{0:T(128)} %get-tuple-element.26.rowmap_ref, f32[16,32,1280]{2,1,0:T(8,128)} %bitcast.31, f32[16,80,1280]{2,1,0:T(8,128)} %sine_dynamic-update-slice_fusion.1.ph_ref), custom_call_target="tpu_custom_call" | custom-call | tf_op jit(solution)/shard_map/pallas_call | solution.py:139
  165.5 8.7 %slice.15 = bf16[16,4,5248]{2,1,0:T(4,128)(2,1)S(1)} slice(bf16[16,16,5248]{2,1,0:T(8,128)(2,1)} %shard_map.77), slice={[0:16:1], [0:16:4], [0:5248:1]} | slice | bytes 1343488 | tf_op jit(solution)/shard_map/slice | solution.py:182
  174.2 0.3 convert_multiply_fusion
  174.5 2.5 %rev.17 = f32[16,4,5248]{2,1,0:T(4,128)S(1)} reverse(f32[16,4,5248]{2,1,0:T(4,128)S(1)} %convert_multiply_fusion), dimensions={1} | reverse | bytes 2686976 | tf_op jit(solution)/shard_map/jit(_flip)/rev | solution.py:190
  177.0 3.5 %reduce_window_sum.11 = f32[16,4,5248]{2,1,0:T(4,128)S(1)} reduce-window(f32[16,4,5248]{2,1,0:T(4,128)S(1)} %rev.17, f32[]{:T(128)} %constant.76.clone.1), window={size=1x4x1 pad=0_0x3_0x0_0}, to_apply=%region_0.1 | reduce-window | flops 1007616 | bytes 2686980 | tf_op jit(solution)/shard_map/jit(cumsum)/reduce_window_sum | solution.py:190
  180.4 0.3 slice.19
  180.8 2.2 %collective-permute-start = (f32[16,5248]{1,0:T(8,128)S(1)}, f32[16,5248]{1,0:T(8,128)S(1)}, u32[]{:S(2)}, u32[]{:S(2)}) collective-permute-start(f32[16,5248]{1,0:T(8,128)S(1)} %bitcast.34), channel_id=1, source_target_pairs={{1,0},{2,1},{3,2},{5,4},{6,5},{7,6},{9,8},{10,9},{11,10},{13,12},{... | collective-permute-start | bytes 1007624 | tf_op jit(solution)/shard_map/ppermute | solution.py:193
  183.0 7.9 %collective-permute-done = f32[16,5248]{1,0:T(8,128)S(1)} collective-permute-done((f32[16,5248]{1,0:T(8,128)S(1)}, f32[16,5248]{1,0:T(8,128)S(1)}, u32[]{:S(2)}, u32[]{:S(2)}) %collective-permute-start) | collective-permute-done | bytes 335904 | tf_op jit(solution)/shard_map/ppermute | solution.py:193
  190.9 0.8 fusion.39
  191.7 1.3 collective-permute-start.1
  192.9 2.5 %rev.18 = f32[16,4,5248]{2,1,0:T(4,128)S(1)} reverse(f32[16,4,5248]{2,1,0:T(4,128)S(1)} %reduce_window_sum.11), dimensions={1} | reverse | bytes 2686976 | tf_op jit(solution)/shard_map/jit(_flip)/rev | solution.py:190
  195.4 7.2 %collective-permute-done.1 = f32[16,5248]{1,0:T(8,128)S(1)} collective-permute-done((f32[16,5248]{1,0:T(8,128)}, f32[16,5248]{1,0:T(8,128)S(1)}, u32[]{:S(2)}, u32[]{:S(2)}) %collective-permute-start.1) | collective-permute-done | bytes 335904 | tf_op jit(solution)/shard_map/ppermute | solution.py:195
  202.6 1.2 add_convert_fusion
  (19 shorter events, 0.1 us)
Async XLA Ops:
  0.6 2.0 copy-start.1
  0.6 2.6 %copy-start.4 = (bf16[2,2]{1,0:T(2,128)(2,1)S(1)}, bf16[2,2]{1,0:T(2,128)(2,1)}, u32[]{:S(2)}) copy-start(bf16[2,2]{1,0:T(2,128)(2,1)} %constant.77.clone) | copy-start | bytes 28
  47.4 12.5 %copy-start.2 = (s32[512]{0:T(512)S(1)}, s32[512]{0:T(512)}, u32[]{:S(2)}) copy-start(s32[512]{0:T(512)} %param.9) | copy-start | bytes 6148
  47.4 13.6 %copy-start.3 = (f32[16]{0:T(128)S(1)}, f32[16]{0:T(128)}, u32[]{:S(2)}) copy-start(f32[16]{0:T(128)} %param.10) | copy-start | bytes 196
  47.4 86.1 %all-to-all-start = ((f32[64,20,512]{2,1,0:T(8,128)}), f32[64,20,512]{2,1,0:T(8,128)S(1)}, u32[]{:S(2)}, u32[]{:S(2)}) async-start(f32[64,20,512]{2,1,0:T(8,128)} %copy.28), calls=%async_computation | async-start | bytes 6291456 | tf_op jit(solution)/shard_map/all_to_all | solution.py:169
  61.0 28.7 %copy-start = (s32[16]{0:T(128)}, s32[16]{0:T(128)S(1)}, u32[]{:S(2)}) copy-start(s32[16]{0:T(128)S(1)} %get-tuple-element.3.lengths_ref) | copy-start | bytes 196
  180.8 10.1 %collective-permute-start = (f32[16,5248]{1,0:T(8,128)S(1)}, f32[16,5248]{1,0:T(8,128)S(1)}, u32[]{:S(2)}, u32[]{:S(2)}) collective-permute-start(f32[16,5248]{1,0:T(8,128)S(1)} %bitcast.34), channel_id=1, source_target_pairs={{1,0},{2,1},{3,2},{5,4},{6,5},{7,6},{9,8},{10,9},{11,10},{13,12},{... | collective-permute-start | bytes 1007624 | tf_op jit(solution)/shard_map/ppermute | solution.py:193
  191.7 10.9 %collective-permute-start.1 = (f32[16,5248]{1,0:T(8,128)}, f32[16,5248]{1,0:T(8,128)S(1)}, u32[]{:S(2)}, u32[]{:S(2)}) collective-permute-start(f32[16,5248]{1,0:T(8,128)} %fusion.39), channel_id=1, source_target_pairs={{2,0},{3,1},{6,4},{7,5},{10,8},{11,9},{14,12},{15,13},{18,16},{19,... | collective-permute-start | bytes 1007624 | tf_op jit(solution)/shard_map/ppermute | solution.py:195

commit v3 on v2

--- a/solution.py
+++ b/solution.py
@@ -79,7 +79,8 @@
         tsin_ref[rows, :] = b * q0c + a * q0s
 
 
-def main_kernel(lengths_ref, rowmap_ref, f_ref, ph_ref, out_ref, tw_ref, base_ref, cos_ref, sin_ref):
+def main_kernel(lengths_ref, rowmap_ref, f_ref, ph_ref, out_ref, heat_ref, tw_ref, base_ref, cos_ref,
+                sin_ref, kept_ref):
     expand(ph_ref, base_ref, cos_ref, sin_ref)
     r = pl.program_id(0)
     points = lengths_ref[r]
@@ -98,29 +99,18 @@
     lane = lax.broadcasted_iota(jnp.int32, (fields, BLOCK), 1)
     for b in range(BLOCKS):
         v = values[fields * b:fields * (b + 1), :]
-        v = jnp.where(lane + BLOCK * b < points, v, 0.0)
-        out_ref[0, :, BLOCK * b:BLOCK * (b + 1)] = v.astype(jnp.bfloat16)
-
-
-def heat_kernel(lengths_ref, rowmap_ref, f_ref, ph_ref, out_ref, tw_ref, base_ref, cos_ref, sin_ref):
-    expand(ph_ref, base_ref, cos_ref, sin_ref)
-    slots = f_ref.shape[2]
-    depth = cos_ref.shape[0]
-    fields = f_ref.shape[1] // 2
-    c = cos_ref[...]
-    s = sin_ref[...]
-    for f in range(fields):
-        re = f_ref[0, f:f + 1, :]
-        im = f_ref[0, fields + f:fields + f + 1, :]
-        rows = slice(depth * f, depth * (f + 1))
-        tw_ref[rows, 0:slots] = (re * c - im * s).astype(jnp.bfloat16)
-        tw_ref[rows, slots:2 * slots] = (re * s + im * c).astype(jnp.bfloat16)
-    out_ref[0] = lax.dot_general(tw_ref[...], base_ref[...], (((1,), (1,)), ((), ())),
-                                 preferred_element_type=jnp.float32)
-
-
-def synth(kernel, fourier, ph, lengths, rowmap, out_rows, out_cols, out_dtype, tw_rows):
+        v = jnp.where(lane + BLOCK * b < points, v, 0.0).astype(jnp.bfloat16)
+        out_ref[0, :, BLOCK * b:BLOCK * (b + 1)] = v
+        kept_ref[fields * b:fields * (b + 1), :] = v.astype(jnp.float32)
+    levels = heat_ref.shape[1]
+    for level in range(levels):
+        heat_ref[0, level] = kept_ref[pl.ds(QUANTITY_COUNT * level, BLOCKS, stride=fields), :]
+
+
+def synth(fourier, ph, lengths, rowmap):
     rows, cols, slots = fourier.shape
+    fields = cols // 2
+    levels = fields // QUANTITY_COUNT
     grid_spec = pltpu.PrefetchScalarGridSpec(
         num_scalar_prefetch=2,
         grid=(rows,),
@@ -128,18 +118,25 @@
             pl.BlockSpec((1, cols, slots), lambda r, n, m: (m[r], 0, 0)),
             pl.BlockSpec((1, ph.shape[1], slots), lambda r, n, m: (r, 0, 0)),
         ],
-        out_specs=pl.BlockSpec((1, out_rows, out_cols), lambda r, n, m: (r, 0, 0)),
+        out_specs=[
+            pl.BlockSpec((1, fields, LCAP), lambda r, n, m: (r, 0, 0)),
+            pl.BlockSpec((1, levels, BLOCKS, BLOCK), lambda r, n, m: (r, 0, 0, 0)),
+        ],
         scratch_shapes=[
-            pltpu.VMEM((tw_rows, 2 * slots), jnp.bfloat16),
+            pltpu.VMEM((fields * BLOCKS, 2 * slots), jnp.bfloat16),
             pltpu.VMEM((BLOCK, 2 * slots), jnp.bfloat16),
             pltpu.VMEM((DEPTH, slots), jnp.float32),
             pltpu.VMEM((DEPTH, slots), jnp.float32),
+            pltpu.VMEM((fields * BLOCKS, BLOCK), jnp.float32),
         ],
     )
     return pl.pallas_call(
-        kernel,
+        main_kernel,
         grid_spec=grid_spec,
-        out_shape=jax.ShapeDtypeStruct((rows, out_rows, out_cols), out_dtype),
+        out_shape=(
+            jax.ShapeDtypeStruct((rows, fields, LCAP), jnp.bfloat16),
+            jax.ShapeDtypeStruct((rows, levels, BLOCKS, BLOCK), jnp.float32),
+        ),
         compiler_params=pltpu.CompilerParams(dimension_semantics=("arbitrary",)),
     )(lengths, rowmap, fourier, ph)
 
@@ -177,9 +174,8 @@
     points_all = jnp.concatenate([row_points, jnp.flip(row_points)])
     lengths = lax.dynamic_slice_in_dim(points_all, wave_rank * band_rows, band_rows)
     ph = tables(wave_numbers, lengths)
-    values = synth(main_kernel, fourier, ph, lengths, rowmap,
-                   fields, LCAP, jnp.bfloat16, fields * BLOCKS)
-    heat_state_values = values[:, 0::QUANTITY_COUNT, :].astype(jnp.float32)
+    values, heat = synth(fourier, ph, lengths, rowmap)
+    heat_state_values = heat.reshape(band_rows, fields // QUANTITY_COUNT, LCAP)
 
     device_layers = heat_state_values.shape[1]
     lev_rank = lax.axis_index("lev")
@@ -187,13 +183,18 @@
         layer_logpressure_factor, lev_rank * device_layers, device_layers
     )
     scaled_heat_values = heat_state_values * layer_depth_factor[None, :, None]
-    partial_totals = jnp.flip(jnp.cumsum(jnp.flip(scaled_heat_values, 1), axis=1), 1)
+    levels = scaled_heat_values.shape[1]
+    running = [scaled_heat_values[:, levels - 1]]
+    for level in range(levels - 2, -1, -1):
+        running.append(scaled_heat_values[:, level] + running[-1])
+    partial_totals = jnp.stack(running[::-1], axis=1)
     lev_count = lax.axis_size("lev")
-    bottom = partial_totals[:, 0, :]
-    next_one = lax.ppermute(bottom, "lev", [(d + 1, d) for d in range(lev_count - 1)])
-    pair_sum = bottom + next_one
-    next_two = lax.ppermute(pair_sum, "lev", [(d + 2, d) for d in range(lev_count - 2)])
-    deeper = next_one + next_two
+    bottom = running[-1]
+    shifted = [lax.ppermute(bottom, "lev", [(d + k, d) for d in range(lev_count - k)])
+               for k in range(1, lev_count)]
+    deeper = shifted[0]
+    for more in shifted[1:]:
+        deeper = deeper + more
     geopotential = (partial_totals + deeper[:, None, :]).astype(jnp.bfloat16)
     return (values, geopotential)
 

time: 206 us -> 188 us (0.913)
  local copies, waits for them, and re-layouts: 46.7 us -> 35.7 us
  other arithmetic: 47.9 us -> 42.5 us
    slice x2 -> x0, local copies, waits for them, and re-layouts: 9.03 us -> none  [the longest x1 8.69 us: local(): heat_state_values = values[:, 0::QUANTITY_COUNT, :].astype(jnp.float32)]
    rev x2 -> x0, local copies, waits for them, and re-layouts: 4.91 us -> none  [the longest x1 2.45 us: local(): jnp.flip(scaled_heat_values, 1)]
    another operation x1 -> x0, other arithmetic: 3.45 us -> none  [local(): jnp.cumsum(jnp.flip(scaled_heat_values, 1), axis=1)]
    ppermute x2 -> x3, starting transfers between devices: 3.49 us -> 5.03 us  [local(): lax.ppermute(bottom, 'lev', [(d + k, d) for d in range(lev_count - k)])]
    ppermute x2 -> x3, waiting for transfers between devices: 15 us -> 14.3 us  [local(): lax.ppermute(bottom, 'lev', [(d + k, d) for d in range(lev_count - k)])]
  transfers between devices with their start and end apart: 3 -> 4, of which waited for: 3 -> 3; matrix products, arithmetic and copies ran while one was open for 17% -> 18% of each run, Pallas kernels for 0% -> 0%
where the time goes in v3:
time: 188 us; the launch traced here: 187 us
  waiting for transfers between devices  55 us (29%)
  other arithmetic  42.5 us (23%)
  local copies, waits for them, and re-layouts  35.7 us (19%)
  Pallas kernels  26.2 us (14%)
  starting transfers between devices  17.4 us (9%)
  matrix products  9.81 us (5%)
    all_to_all x1, waiting for transfers between devices, local(): got = lax.all_to_all(send, 'wave', 0, 0, tiled=True)  40.6 us
    unnamed x7, other arithmetic  28.3 us
    pallas_call x1, Pallas kernels, synth(): pl.pallas_call(main_kernel, grid_spec=grid_spec, out_shape=(jax.ShapeDtyp...  26.2 us
    ppermute x3, waiting for transfers between devices, local(): lax.ppermute(bottom, 'lev', [(d + k, d) for d in range(lev_count - k)])  14.3 us
    all_to_all x1, starting transfers between devices, local(): got = lax.all_to_all(send, 'wave', 0, 0, tiled=True)  12.4 us
    dot_general x1, matrix products, local(): jnp.einsum('qaehci,qeit->qahct', lhs, legendre, preferred_element_type=jn...  9.81 us
    transpose x1, local copies, waits for them, and re-layouts, local(): bands.transpose(3, 0, 1, 4, 2)  9.47 us
    transpose x1, other arithmetic, local(): bands.transpose(3, 0, 1, 4, 2)  9.14 us
  transfers between devices with their start and end apart: 4, of which 3 were waited for; matrix products, arithmetic and copies ran while one was open for 18% of the time, Pallas kernels for 0%

profile of v3, /device:TPU:2, one launch (start us, length us, event | category | flops | bytes accessed | tf_op | source)
XLA Modules:
  0.0 187.5 jit_solution(5472301822492772062)
XLA Ops:
  0.6 0.0 copy-start.1
  0.6 1.9 %copy.27 = bf16[10,2,32,640]{3,1,2,0:T(2,128)(2,1)S(1)} copy(bf16[10,2,32,640]{3,2,1,0:T(8,128)(2,1)} %param.6) | data formatting | bytes 1638400 | tf_op args[0]
  2.5 0.1 copy.28
  2.7 0.0 copy-start.4
  2.7 0.1 broadcast_subtract_fusion.1
  2.8 0.1 fusion.31
  2.8 0.1 iota_compare_fusion
  3.0 0.1 add_convert_fusion
  3.1 0.2 broadcast_multiply_fusion
  3.3 0.0 copy-done.4
  3.3 9.8 %fusion = f32[10,2,2,32,512,1]{3,4,5,2,1,0:T(8,128)S(1)} fusion(bf16[10,2,640,512]{3,2,1,0:T(8,128)(2,1)} %param.7, bf16[10,2,2,32,640]{4,3,1,2,0:T(8,128)(2,1)S(1)} %broadcast_multiply_fusion, bf16[2,2]{1,0:T(2,128)(2,1)S(1)} %copy-done.4), kind=kOutput, calls=%fused_computation | convolution fusion | flops 1679360000 | bytes 17367048 | tf_op jit(solution)/shard_map/qaehci,qeit->qahct/dot_general | solution.py:160
  13.1 4.7 %slice_bitcast_fusion.1 = (f32[10,2,32,32,16]{2,4,3,1,0:T(8,128)}, f32[10,2,32,32,16]{2,4,3,1,0:T(8,128)}) fusion(f32[10,2,2,32,32,16]{3,5,4,2,1,0:T(8,128)S(1)} %bitcast.26), kind=kLoop, calls=%fused_computation.4 | loop fusion | bytes 5242880 | tf_op jit(solution)/shard_map/squeeze | solution.py:162
  17.8 5.2 %rev.9 = f32[10,2,32,32,16]{2,4,3,1,0:T(8,128)} reverse(f32[10,2,32,32,16]{2,4,3,1,0:T(8,128)} %get-tuple-element.20), dimensions={3} | reverse | bytes 2621440 | tf_op jit(solution)/shard_map/jit(_flip)/rev | solution.py:163
  23.1 9.1 %maximum_bitcast_fusion = f32[64,10,2,16,32]{4,3,0,2,1:T(8,128)} fusion(f32[10,2,32,32,16]{2,4,3,1,0:T(8,128)} %rev.9, f32[10,2,32,32,16]{2,4,3,1,0:T(8,128)} %get-tuple-element.19), kind=kLoop, calls=%fused_computation.2 | loop fusion | flops 655360 | bytes 5242880 | tf_op jit(solution)/shard_map/transpose | solution.py:165
  32.2 9.5 %copy.31 = f32[64,10,2,16,32]{0,4,3,2,1:T(8,128)} copy(f32[64,10,2,16,32]{4,3,0,2,1:T(8,128)} %maximum_bitcast_fusion) | data formatting | bytes 5242880 | tf_op jit(solution)/shard_map/transpose | solution.py:165
  41.7 5.8 %copy.32 = f32[64,20,512]{2,1,0:T(8,128)} copy(f32[64,20,512]{0,2,1:T(8,128)} %bitcast.24) | data formatting | bytes 5242880 | tf_op jit(solution)/shard_map/reshape | solution.py:165
  47.5 12.4 %all-to-all-start = ((f32[64,20,512]{2,1,0:T(8,128)}), f32[64,20,512]{2,1,0:T(8,128)S(1)}, u32[]{:S(2)}, u32[]{:S(2)}) async-start(f32[64,20,512]{2,1,0:T(8,128)} %copy.32), calls=%async_computation | async-start | bytes 6291456 | tf_op jit(solution)/shard_map/all_to_all | solution.py:166
  60.0 0.1 rev.8
  60.1 0.2 copy.34
  60.3 0.2 mul.246
  60.5 0.5 fusion.39
  61.0 0.1 compare_convert_fusion
  61.1 0.1 dynamic_slice.11
  61.2 0.1 broadcast_multiply_fusion.1
  61.3 5.9 %cosine_dynamic-update-slice_fusion = f32[16,80,1280]{2,1,0:T(8,128)} fusion(f32[16]{0:T(128)S(1)} %broadcast_divide_fusion, s32[16]{0:T(128)S(1)} %get-tuple-element.16.lengths_ref, f32[16]{0:T(128)S(1)} %convert_element_type.90, f32[16,1280]{1,0:T(8,128)S(1)} %get-tuple-element.33, s32[16,1280]{1,0:T(8,128)S(1)} %get-tuple-element.32), kind=kLoop, calls=%fused_computation.26 | loop fusion | flops 4259839 | bytes 1474752
  67.2 5.9 %sine_dynamic-update-slice_fusion = f32[16,80,1280]{2,1,0:T(8,128)} fusion(f32[16,80,1280]{2,1,0:T(8,128)} %cosine_dynamic-update-slice_fusion, f32[16]{0:T(128)S(1)} %broadcast_divide_fusion, s32[16]{0:T(128)S(1)} %get-tuple-element.16.lengths_ref, f32[16]{0:T(128)S(1)} %convert_element_type.90, f32[16,1280]{1,0:T(8,128)S(1)} %get-tuple-element.33, ...), kind=kLoop, calls=%fused_computation.25 | loop fusion | flops 4259840 | bytes 1474752
  73.0 3.3 %cosine_dynamic-update-slice_fusion.2 = f32[16,80,1280]{2,1,0:T(8,128)} fusion(f32[16,80,1280]{2,1,0:T(8,128)} %sine_dynamic-update-slice_fusion, f32[16]{0:T(128)S(1)} %broadcast_divide_fusion, s32[16]{0:T(128)S(1)} %get-tuple-element.16.lengths_ref, f32[16]{0:T(128)S(1)} %convert_element_type.90, f32[8,1280]{1,0:T(8,128)S(1)} %get-tuple-element.30, ...), kind=kLoop, calls=%fused_computation.51 | loop fusion | flops 2129920 | bytes 737472
  76.3 3.3 %sine_dynamic-update-slice_fusion.2 = f32[16,80,1280]{2,1,0:T(8,128)} fusion(f32[16,80,1280]{2,1,0:T(8,128)} %cosine_dynamic-update-slice_fusion.2, f32[16]{0:T(128)S(1)} %broadcast_divide_fusion, s32[16]{0:T(128)S(1)} %get-tuple-element.16.lengths_ref, f32[16]{0:T(128)S(1)} %convert_element_type.90, f32[8,1280]{1,0:T(8,128)S(1)} %get-tuple-element.30, ...), kind=kLoop, calls=%fused_computation.50 | loop fusion | flops 2129920 | bytes 737472
  79.6 3.3 %multiply_dynamic-update-slice_fusion.1 = f32[16,80,1280]{2,1,0:T(8,128)} fusion(f32[16,80,1280]{2,1,0:T(8,128)} %sine_dynamic-update-slice_fusion.2, f32[16,1280]{1,0:T(8,128)S(1)} %compare_convert_fusion, f32[16]{0:T(128)S(1)} %broadcast_divide_fusion, s32[16]{0:T(128)S(1)} %get-tuple-element.16.lengths_ref, f32[16]{0:T(128)S(1)} %convert_element_type.90, ...), kind=kLoop, calls=%fused_computation.49 | loop fusion | flops 2293760 | bytes 819392
  83.0 3.4 %multiply_dynamic-update-slice_fusion = f32[16,80,1280]{2,1,0:T(8,128)} fusion(f32[16,80,1280]{2,1,0:T(8,128)} %multiply_dynamic-update-slice_fusion.1, f32[16,1280]{1,0:T(8,128)S(1)} %compare_convert_fusion, f32[16]{0:T(128)S(1)} %broadcast_divide_fusion, s32[16]{0:T(128)S(1)} %get-tuple-element.16.lengths_ref, f32[16]{0:T(128)S(1)} %convert_element_type.90, ...), kind=kLoop, calls=%fused_computation.48 | loop fusion | flops 2293760 | bytes 819392
  86.3 3.3 %cosine_dynamic-update-slice_fusion.1 = f32[16,80,1280]{2,1,0:T(8,128)} fusion(f32[16,80,1280]{2,1,0:T(8,128)} %multiply_dynamic-update-slice_fusion, f32[16]{0:T(128)S(1)} %broadcast_divide_fusion, s32[16]{0:T(128)S(1)} %get-tuple-element.16.lengths_ref, f32[16]{0:T(128)S(1)} %convert_element_type.90, f32[8,1280]{1,0:T(8,128)S(1)} %get-tuple-element.23, ...), kind=kLoop, calls=%fused_computation.47 | loop fusion | flops 2129920 | bytes 737472
  89.6 3.3 %sine_dynamic-update-slice_fusion.1.ph_ref = f32[16,80,1280]{2,1,0:T(8,128)} fusion(f32[16,80,1280]{2,1,0:T(8,128)} %cosine_dynamic-update-slice_fusion.1, f32[16]{0:T(128)S(1)} %broadcast_divide_fusion, s32[16]{0:T(128)S(1)} %get-tuple-element.16.lengths_ref, f32[16]{0:T(128)S(1)} %convert_element_type.90, f32[8,1280]{1,0:T(8,128)S(1)} %get-tuple-element.23, ...), kind=kLoop, calls=%fused_computation.46 | loop fusion | flops 2129920 | bytes 737472 | tf_op jit(solution)/shard_map/concatenate | solution.py:57
  93.0 40.6 %all-to-all-done = f32[64,20,512]{2,1,0:T(8,128)S(1)} async-done(((f32[64,20,512]{2,1,0:T(8,128)}), f32[64,20,512]{2,1,0:T(8,128)S(1)}, u32[]{:S(2)}, u32[]{:S(2)}) %all-to-all-start) | async-done | bytes 2621472 | tf_op jit(solution)/shard_map/all_to_all | solution.py:166
  133.6 1.6 reshape.454
  135.2 3.3 %copy.33 = f32[512,1280]{1,0:T(8,128)} copy(f32[512,1280]{0,1:T(8,128)} %bitcast.27) | data formatting | bytes 5242880 | tf_op jit(solution)/shard_map/transpose | solution.py:168
  138.5 26.2 %shard_map.77 = (bf16[16,16,5248]{2,1,0:T(8,128)(2,1)}, f32[16,4,41,128]{3,2,1,0:T(8,128)}) custom-call(s32[16]{0:T(128)} %copy-done, s32[16]{0:T(128)} %get-tuple-element.40.rowmap_ref, f32[16,32,1280]{2,1,0:T(8,128)} %bitcast.25, f32[16,80,1280]{2,1,0:T(8,128)} %sine_dynamic-update-slice_fusion.1.ph_ref), custom_call_target="tpu_custom_call" | custom-call | tf_op jit(solution)/shard_map/pallas_call | solution.py:133
  164.7 1.8 reshape.459
  166.5 0.2 copy_multiply_fusion
  166.7 0.1 slice_add_fusion.2
  166.8 0.7 collective-permute-start.2
  167.5 3.1 %collective-permute-start = (f32[16,5248]{1,0:T(8,128)S(1)}, f32[16,5248]{1,0:T(8,128)S(1)}, u32[]{:S(2)}, u32[]{:S(2)}) collective-permute-start(f32[16,5248]{1,0:T(8,128)S(1)} %bitcast.31), channel_id=1, source_target_pairs={{1,0},{2,1},{3,2},{5,4},{6,5},{7,6},{9,8},{10,9},{11,10},{13,12},{... | collective-permute-start | bytes 1007624 | tf_op jit(solution)/shard_map/ppermute | solution.py:193
  170.6 1.3 collective-permute-start.1
  171.9 0.0 collective-permute-done.2
  171.9 7.1 %collective-permute-done = f32[16,5248]{1,0:T(8,128)S(1)} collective-permute-done((f32[16,5248]{1,0:T(8,128)S(1)}, f32[16,5248]{1,0:T(8,128)S(1)}, u32[]{:S(2)}, u32[]{:S(2)}) %collective-permute-start) | collective-permute-done | bytes 335904 | tf_op jit(solution)/shard_map/ppermute | solution.py:193
  178.9 7.3 %collective-permute-done.1 = f32[16,5248]{1,0:T(8,128)S(1)} collective-permute-done((f32[16,5248]{1,0:T(8,128)S(1)}, f32[16,5248]{1,0:T(8,128)S(1)}, u32[]{:S(2)}, u32[]{:S(2)}) %collective-permute-start.1) | collective-permute-done | bytes 335904 | tf_op jit(solution)/shard_map/ppermute | solution.py:193
  186.2 0.1 add_add_fusion
  186.3 0.1 fusion.5
  186.4 1.1 copy.36
  (17 shorter events, 0.1 us)
Async XLA Ops:
  0.6 2.0 %copy-start.1 = (s32[640]{0:T(1024)S(1)}, s32[640]{0:T(1024)}, u32[]{:S(2)}) copy-start(s32[640]{0:T(1024)} %param.8) | copy-start | bytes 7684
  2.7 0.7 copy-start.4
  47.5 12.5 %copy-start.2 = (s32[512]{0:T(512)S(1)}, s32[512]{0:T(512)}, u32[]{:S(2)}) copy-start(s32[512]{0:T(512)} %param.9) | copy-start | bytes 6148
  47.5 13.6 %copy-start.3 = (f32[16]{0:T(128)S(1)}, f32[16]{0:T(128)}, u32[]{:S(2)}) copy-start(f32[16]{0:T(128)} %param.10) | copy-start | bytes 196
  47.5 86.1 %all-to-all-start = ((f32[64,20,512]{2,1,0:T(8,128)}), f32[64,20,512]{2,1,0:T(8,128)S(1)}, u32[]{:S(2)}, u32[]{:S(2)}) async-start(f32[64,20,512]{2,1,0:T(8,128)} %copy.32), calls=%async_computation | async-start | bytes 6291456 | tf_op jit(solution)/shard_map/all_to_all | solution.py:166
  61.0 28.6 %copy-start = (s32[16]{0:T(128)}, s32[16]{0:T(128)S(1)}, u32[]{:S(2)}) copy-start(s32[16]{0:T(128)S(1)} %get-tuple-element.16.lengths_ref) | copy-start | bytes 196
  166.8 5.1 %collective-permute-start.2 = (f32[16,5248]{1,0:T(8,128)S(1)}, f32[16,5248]{1,0:T(8,128)S(1)}, u32[]{:S(2)}, u32[]{:S(2)}) collective-permute-start(f32[16,5248]{1,0:T(8,128)S(1)} %bitcast.30), channel_id=1, source_target_pairs={{3,0},{7,4},{11,8},{15,12},{19,16},{23,20},{27,24},{31,28},{35,32}... | collective-permute-start | bytes 1007624 | tf_op jit(solution)/shard_map/ppermute | solution.py:193
  167.5 11.4 %collective-permute-start = (f32[16,5248]{1,0:T(8,128)S(1)}, f32[16,5248]{1,0:T(8,128)S(1)}, u32[]{:S(2)}, u32[]{:S(2)}) collective-permute-start(f32[16,5248]{1,0:T(8,128)S(1)} %bitcast.31), channel_id=1, source_target_pairs={{1,0},{2,1},{3,2},{5,4},{6,5},{7,6},{9,8},{10,9},{11,10},{13,12},{... | collective-permute-start | bytes 1007624 | tf_op jit(solution)/shard_map/ppermute | solution.py:193
  170.6 15.6 %collective-permute-start.1 = (f32[16,5248]{1,0:T(8,128)S(1)}, f32[16,5248]{1,0:T(8,128)S(1)}, u32[]{:S(2)}, u32[]{:S(2)}) collective-permute-start(f32[16,5248]{1,0:T(8,128)S(1)} %bitcast.32), channel_id=1, source_target_pairs={{2,0},{3,1},{6,4},{7,5},{10,8},{11,9},{14,12},{15,13},{18,16},{19,... | collective-permute-start | bytes 1007624 | tf_op jit(solution)/shard_map/ppermute | solution.py:193

commit v4 on v3

--- a/solution.py
+++ b/solution.py
@@ -157,12 +157,10 @@
     selected = coef[:, :, None, :, :] * selection[:, :, :, None, :]
     signs = jnp.array([[1.0, 1.0], [1.0, -1.0]], jnp.bfloat16)
     lhs = signs[None, :, :, None, None, None] * selected[:, None]
-    sums = jnp.einsum("qaehci,qeit->qahct", lhs, legendre, preferred_element_type=jnp.float32)
-    sums = sums.reshape(pair_local, 2, 2, cols, half_bands, band_rows)
-    north = sums[:, 0]
-    south = jnp.flip(sums[:, 1], 3)
-    bands = jnp.concatenate([north, south], 3)
-    send = bands.transpose(3, 0, 1, 4, 2).reshape(wave_count, pair_local * 2, band_rows * cols)
+    sums = jnp.einsum("qaehci,qeit->atqhc", lhs, legendre, preferred_element_type=jnp.float32)
+    sums = sums.reshape(2, half_bands, band_rows, pair_local, 2, cols)
+    bands = jnp.concatenate([sums[0], jnp.flip(sums[1], 0)], 0)
+    send = bands.transpose(0, 2, 3, 1, 4).reshape(wave_count, pair_local * 2, band_rows * cols)
     got = lax.all_to_all(send, "wave", 0, 0, tiled=True)
     slots = got.shape[0] * got.shape[1]
     fourier = got.reshape(slots, band_rows * cols).T.reshape(band_rows, cols, slots)

time: 188 us -> 188 us (level)
  matrix products: 9.81 us -> 6.65 us
  local copies, waits for them, and re-layouts: 35.7 us -> 38.7 us
    slice x0 -> x3, local copies, waits for them, and re-layouts: none -> 7.58 us  [local(): bands = jnp.concatenate([sums[0], jnp.flip(sums[1], 0)], 0)]
    squeeze x1 -> x0, local copies, waits for them, and re-layouts: 4.7 us -> none  [local(): north = sums[:, 0]]
    dot_general x1, matrix products: 9.81 us -> 6.65 us  [local(): jnp.einsum('qaehci,qeit->atqhc', lhs, legendre, preferred_element_type=jn...]
where the time goes in v4:
time: 188 us; the launch traced here: 187 us
  waiting for transfers between devices  55.2 us (29%)
  other arithmetic  42.5 us (23%)
  local copies, waits for them, and re-layouts  38.7 us (21%)
  Pallas kernels  26.2 us (14%)
  starting transfers between devices  17.2 us (9%)
  matrix products  6.65 us (4%)
    all_to_all x1, waiting for transfers between devices, local(): got = lax.all_to_all(send, 'wave', 0, 0, tiled=True)  40.6 us
    unnamed x7, other arithmetic  28.3 us
    pallas_call x1, Pallas kernels, synth(): pl.pallas_call(main_kernel, grid_spec=grid_spec, out_shape=(jax.ShapeDtyp...  26.2 us
    ppermute x3, waiting for transfers between devices, local(): lax.ppermute(bottom, 'lev', [(d + k, d) for d in range(lev_count - k)])  14.6 us
    all_to_all x1, starting transfers between devices, local(): got = lax.all_to_all(send, 'wave', 0, 0, tiled=True)  12.4 us
    transpose x1, local copies, waits for them, and re-layouts, local(): bands.transpose(0, 2, 3, 1, 4)  9.47 us
    transpose x1, other arithmetic, local(): bands.transpose(0, 2, 3, 1, 4)  9.14 us
    slice x3, local copies, waits for them, and re-layouts, local(): bands = jnp.concatenate([sums[0], jnp.flip(sums[1], 0)], 0)  7.58 us
  transfers between devices with their start and end apart: 4, of which 3 were waited for; matrix products, arithmetic and copies ran while one was open for 18% of the time, Pallas kernels for 0%

profile of v4, /device:TPU:2, one launch (start us, length us, event | category | flops | bytes accessed | tf_op | source)
XLA Modules:
  0.0 187.3 jit_solution(11595067129938760974)
XLA Ops:
  0.6 1.9 %copy.26 = bf16[10,2,32,640]{3,1,2,0:T(2,128)(2,1)S(1)} copy(bf16[10,2,32,640]{3,2,1,0:T(8,128)(2,1)} %param.6) | data formatting | bytes 1638400 | tf_op args[0]
  2.5 0.1 copy.27
  2.7 0.0 copy-start
  2.7 0.1 broadcast_subtract_fusion.1
  2.8 0.1 fusion.36
  2.8 0.1 iota_compare_fusion
  3.0 0.1 add_convert_fusion
  3.1 0.2 broadcast_multiply_fusion
  3.3 0.0 copy-done
  3.3 6.6 %fusion.3 = f32[2,512,10,2,32]{1,4,3,0,2:T(8,128)S(1)} fusion(bf16[10,2,640,512]{3,2,1,0:T(8,128)(2,1)} %param.7, bf16[10,2,2,32,640]{4,3,1,2,0:T(8,128)(2,1)S(1)} %broadcast_multiply_fusion, bf16[2,2]{1,0:T(2,128)(2,1)S(1)} %copy-done), kind=kOutput, calls=%fused_computation.12 | convolution fusion | flops 1679360000 | bytes 17367048 | tf_op jit(solution)/shard_map/qaehci,qeit->atqhc/dot_general | solution.py:160
  10.0 0.3 fusion.45
  10.3 3.7 %copy.29 = f32[1,512,10,2,32]{4,1,3,2,0:T(8,128)} copy(f32[1,512,10,2,32]{1,4,3,0,2:T(8,128)S(1)} %get-tuple-element.20) | data formatting | bytes 2621440 | tf_op jit(solution)/shard_map/slice | solution.py:162
  13.9 5.3 %rev.9 = f32[32,16,10,2,32]{4,1,0,3,2:T(8,128)} reverse(f32[32,16,10,2,32]{4,1,0,3,2:T(8,128)} %bitcast.25), dimensions={0} | reverse | bytes 2621440 | tf_op jit(solution)/shard_map/jit(_flip)/rev | solution.py:162
  19.3 3.6 %copy.28 = f32[1,512,10,2,32]{4,1,3,2,0:T(8,128)} copy(f32[1,512,10,2,32]{1,4,3,0,2:T(8,128)S(1)} %get-tuple-element.19) | data formatting | bytes 2621440 | tf_op jit(solution)/shard_map/slice | solution.py:162
  22.9 9.1 %maximum_bitcast_fusion = f32[64,10,2,16,32]{4,3,0,2,1:T(8,128)} fusion(f32[32,16,10,2,32]{4,1,0,3,2:T(8,128)} %rev.9, f32[32,16,10,2,32]{4,1,0,3,2:T(8,128)} %bitcast.24), kind=kLoop, calls=%fused_computation.2 | loop fusion | flops 655360 | bytes 5242880 | tf_op jit(solution)/shard_map/transpose | solution.py:163
  32.0 9.5 %copy.30 = f32[64,10,2,16,32]{0,4,3,2,1:T(8,128)} copy(f32[64,10,2,16,32]{4,3,0,2,1:T(8,128)} %maximum_bitcast_fusion) | data formatting | bytes 5242880 | tf_op jit(solution)/shard_map/transpose | solution.py:163
  41.5 5.8 %copy.31 = f32[64,20,512]{2,1,0:T(8,128)} copy(f32[64,20,512]{0,2,1:T(8,128)} %bitcast.26) | data formatting | bytes 5242880 | tf_op jit(solution)/shard_map/reshape | solution.py:163
  47.3 12.4 %all-to-all-start = ((f32[64,20,512]{2,1,0:T(8,128)}), f32[64,20,512]{2,1,0:T(8,128)S(1)}, u32[]{:S(2)}, u32[]{:S(2)}) async-start(f32[64,20,512]{2,1,0:T(8,128)} %copy.31), calls=%async_computation | async-start | bytes 6291456 | tf_op jit(solution)/shard_map/all_to_all | solution.py:164
  59.8 0.1 rev.8
  59.9 0.2 copy.33
  60.1 0.2 mul.246
  60.3 0.5 fusion.44
  60.9 0.1 compare_convert_fusion
  61.0 0.1 dynamic_slice.11
  61.1 0.1 broadcast_multiply_fusion.1
  61.2 5.9 %cosine_dynamic-update-slice_fusion = f32[16,80,1280]{2,1,0:T(8,128)} fusion(f32[16]{0:T(128)S(1)} %broadcast_divide_fusion, s32[16]{0:T(128)S(1)} %get-tuple-element.16.lengths_ref, f32[16]{0:T(128)S(1)} %convert_element_type.90, f32[16,1280]{1,0:T(8,128)S(1)} %get-tuple-element.33, s32[16,1280]{1,0:T(8,128)S(1)} %get-tuple-element.32), kind=kLoop, calls=%fused_computation.25 | loop fusion | flops 4259839 | bytes 1474752
  67.0 5.9 %sine_dynamic-update-slice_fusion = f32[16,80,1280]{2,1,0:T(8,128)} fusion(f32[16,80,1280]{2,1,0:T(8,128)} %cosine_dynamic-update-slice_fusion, f32[16]{0:T(128)S(1)} %broadcast_divide_fusion, s32[16]{0:T(128)S(1)} %get-tuple-element.16.lengths_ref, f32[16]{0:T(128)S(1)} %convert_element_type.90, f32[16,1280]{1,0:T(8,128)S(1)} %get-tuple-element.33, ...), kind=kLoop, calls=%fused_computation.24 | loop fusion | flops 4259840 | bytes 1474752
  72.9 3.3 %cosine_dynamic-update-slice_fusion.2 = f32[16,80,1280]{2,1,0:T(8,128)} fusion(f32[16,80,1280]{2,1,0:T(8,128)} %sine_dynamic-update-slice_fusion, f32[16]{0:T(128)S(1)} %broadcast_divide_fusion, s32[16]{0:T(128)S(1)} %get-tuple-element.16.lengths_ref, f32[16]{0:T(128)S(1)} %convert_element_type.90, f32[8,1280]{1,0:T(8,128)S(1)} %get-tuple-element.30, ...), kind=kLoop, calls=%fused_computation.50 | loop fusion | flops 2129920 | bytes 737472
  76.2 3.3 %sine_dynamic-update-slice_fusion.2 = f32[16,80,1280]{2,1,0:T(8,128)} fusion(f32[16,80,1280]{2,1,0:T(8,128)} %cosine_dynamic-update-slice_fusion.2, f32[16]{0:T(128)S(1)} %broadcast_divide_fusion, s32[16]{0:T(128)S(1)} %get-tuple-element.16.lengths_ref, f32[16]{0:T(128)S(1)} %convert_element_type.90, f32[8,1280]{1,0:T(8,128)S(1)} %get-tuple-element.30, ...), kind=kLoop, calls=%fused_computation.49 | loop fusion | flops 2129920 | bytes 737472
  79.5 3.3 %multiply_dynamic-update-slice_fusion.1 = f32[16,80,1280]{2,1,0:T(8,128)} fusion(f32[16,80,1280]{2,1,0:T(8,128)} %sine_dynamic-update-slice_fusion.2, f32[16,1280]{1,0:T(8,128)S(1)} %compare_convert_fusion, f32[16]{0:T(128)S(1)} %broadcast_divide_fusion, s32[16]{0:T(128)S(1)} %get-tuple-element.16.lengths_ref, f32[16]{0:T(128)S(1)} %convert_element_type.90, ...), kind=kLoop, calls=%fused_computation.48 | loop fusion | flops 2293760 | bytes 819392
  82.8 3.4 %multiply_dynamic-update-slice_fusion = f32[16,80,1280]{2,1,0:T(8,128)} fusion(f32[16,80,1280]{2,1,0:T(8,128)} %multiply_dynamic-update-slice_fusion.1, f32[16,1280]{1,0:T(8,128)S(1)} %compare_convert_fusion, f32[16]{0:T(128)S(1)} %broadcast_divide_fusion, s32[16]{0:T(128)S(1)} %get-tuple-element.16.lengths_ref, f32[16]{0:T(128)S(1)} %convert_element_type.90, ...), kind=kLoop, calls=%fused_computation.47 | loop fusion | flops 2293760 | bytes 819392
  86.1 3.3 %cosine_dynamic-update-slice_fusion.1 = f32[16,80,1280]{2,1,0:T(8,128)} fusion(f32[16,80,1280]{2,1,0:T(8,128)} %multiply_dynamic-update-slice_fusion, f32[16]{0:T(128)S(1)} %broadcast_divide_fusion, s32[16]{0:T(128)S(1)} %get-tuple-element.16.lengths_ref, f32[16]{0:T(128)S(1)} %convert_element_type.90, f32[8,1280]{1,0:T(8,128)S(1)} %get-tuple-element.23, ...), kind=kLoop, calls=%fused_computation.46 | loop fusion | flops 2129920 | bytes 737472
  89.5 3.3 %sine_dynamic-update-slice_fusion.1.ph_ref = f32[16,80,1280]{2,1,0:T(8,128)} fusion(f32[16,80,1280]{2,1,0:T(8,128)} %cosine_dynamic-update-slice_fusion.1, f32[16]{0:T(128)S(1)} %broadcast_divide_fusion, s32[16]{0:T(128)S(1)} %get-tuple-element.16.lengths_ref, f32[16]{0:T(128)S(1)} %convert_element_type.90, f32[8,1280]{1,0:T(8,128)S(1)} %get-tuple-element.23, ...), kind=kLoop, calls=%fused_computation.45 | loop fusion | flops 2129920 | bytes 737472 | tf_op jit(solution)/shard_map/concatenate | solution.py:57
  92.8 40.6 %all-to-all-done = f32[64,20,512]{2,1,0:T(8,128)S(1)} async-done(((f32[64,20,512]{2,1,0:T(8,128)}), f32[64,20,512]{2,1,0:T(8,128)S(1)}, u32[]{:S(2)}, u32[]{:S(2)}) %all-to-all-start) | async-done | bytes 2621472 | tf_op jit(solution)/shard_map/all_to_all | solution.py:164
  133.4 1.6 reshape.455
  135.1 3.3 %copy.32 = f32[512,1280]{1,0:T(8,128)} copy(f32[512,1280]{0,1:T(8,128)} %bitcast.28) | data formatting | bytes 5242880 | tf_op jit(solution)/shard_map/transpose | solution.py:166
  138.4 26.2 %shard_map.77 = (bf16[16,16,5248]{2,1,0:T(8,128)(2,1)}, f32[16,4,41,128]{3,2,1,0:T(8,128)}) custom-call(s32[16]{0:T(128)} %copy-done.1, s32[16]{0:T(128)} %get-tuple-element.40.rowmap_ref, f32[16,32,1280]{2,1,0:T(8,128)} %bitcast.27, f32[16,80,1280]{2,1,0:T(8,128)} %sine_dynamic-update-slice_fusion.1.ph_ref), custom_call_target="tpu_custom_call" | custom-call | tf_op jit(solution)/shard_map/pallas_call | solution.py:133
  164.5 1.8 reshape.460
  166.4 0.2 copy_multiply_fusion
  166.5 0.1 slice_add_fusion.2
  166.6 0.7 collective-permute-start.2
  167.3 2.8 %collective-permute-start = (f32[16,5248]{1,0:T(8,128)S(1)}, f32[16,5248]{1,0:T(8,128)S(1)}, u32[]{:S(2)}, u32[]{:S(2)}) collective-permute-start(f32[16,5248]{1,0:T(8,128)S(1)} %bitcast.32), channel_id=1, source_target_pairs={{1,0},{2,1},{3,2},{5,4},{6,5},{7,6},{9,8},{10,9},{11,10},{13,12},{... | collective-permute-start | bytes 1007624 | tf_op jit(solution)/shard_map/ppermute | solution.py:191
  170.2 1.3 collective-permute-start.1
  171.5 7.1 %collective-permute-done = f32[16,5248]{1,0:T(8,128)S(1)} collective-permute-done((f32[16,5248]{1,0:T(8,128)S(1)}, f32[16,5248]{1,0:T(8,128)S(1)}, u32[]{:S(2)}, u32[]{:S(2)}) %collective-permute-start) | collective-permute-done | bytes 335904 | tf_op jit(solution)/shard_map/ppermute | solution.py:191
  178.5 7.5 %collective-permute-done.1 = f32[16,5248]{1,0:T(8,128)S(1)} collective-permute-done((f32[16,5248]{1,0:T(8,128)S(1)}, f32[16,5248]{1,0:T(8,128)S(1)}, u32[]{:S(2)}, u32[]{:S(2)}) %collective-permute-start.1) | collective-permute-done | bytes 335904 | tf_op jit(solution)/shard_map/ppermute | solution.py:191
  186.1 0.1 add_add_fusion
  186.1 0.1 fusion.10
  186.2 1.1 copy.35
  (19 shorter events, 0.1 us)
Async XLA Ops:
  0.6 2.0 %copy-start.2 = (s32[640]{0:T(1024)S(1)}, s32[640]{0:T(1024)}, u32[]{:S(2)}) copy-start(s32[640]{0:T(1024)} %param.8) | copy-start | bytes 7684
  2.7 0.7 copy-start
  47.3 12.5 %copy-start.3 = (s32[512]{0:T(512)S(1)}, s32[512]{0:T(512)}, u32[]{:S(2)}) copy-start(s32[512]{0:T(512)} %param.9) | copy-start | bytes 6148
  47.3 13.6 %copy-start.4 = (f32[16]{0:T(128)S(1)}, f32[16]{0:T(128)}, u32[]{:S(2)}) copy-start(f32[16]{0:T(128)} %param.10) | copy-start | bytes 196
  47.3 86.1 %all-to-all-start = ((f32[64,20,512]{2,1,0:T(8,128)}), f32[64,20,512]{2,1,0:T(8,128)S(1)}, u32[]{:S(2)}, u32[]{:S(2)}) async-start(f32[64,20,512]{2,1,0:T(8,128)} %copy.31), calls=%async_computation | async-start | bytes 6291456 | tf_op jit(solution)/shard_map/all_to_all | solution.py:164
  60.9 28.6 %copy-start.1 = (s32[16]{0:T(128)}, s32[16]{0:T(128)S(1)}, u32[]{:S(2)}) copy-start(s32[16]{0:T(128)S(1)} %get-tuple-element.16.lengths_ref) | copy-start | bytes 196
  166.6 4.8 %collective-permute-start.2 = (f32[16,5248]{1,0:T(8,128)S(1)}, f32[16,5248]{1,0:T(8,128)S(1)}, u32[]{:S(2)}, u32[]{:S(2)}) collective-permute-start(f32[16,5248]{1,0:T(8,128)S(1)} %bitcast.31), channel_id=1, source_target_pairs={{3,0},{7,4},{11,8},{15,12},{19,16},{23,20},{27,24},{31,28},{35,32}... | collective-permute-start | bytes 1007624 | tf_op jit(solution)/shard_map/ppermute | solution.py:191
  167.3 11.2 %collective-permute-start = (f32[16,5248]{1,0:T(8,128)S(1)}, f32[16,5248]{1,0:T(8,128)S(1)}, u32[]{:S(2)}, u32[]{:S(2)}) collective-permute-start(f32[16,5248]{1,0:T(8,128)S(1)} %bitcast.32), channel_id=1, source_target_pairs={{1,0},{2,1},{3,2},{5,4},{6,5},{7,6},{9,8},{10,9},{11,10},{13,12},{... | collective-permute-start | bytes 1007624 | tf_op jit(solution)/shard_map/ppermute | solution.py:191
  170.2 15.9 %collective-permute-start.1 = (f32[16,5248]{1,0:T(8,128)S(1)}, f32[16,5248]{1,0:T(8,128)S(1)}, u32[]{:S(2)}, u32[]{:S(2)}) collective-permute-start(f32[16,5248]{1,0:T(8,128)S(1)} %bitcast.33), channel_id=1, source_target_pairs={{2,0},{3,1},{6,4},{7,5},{10,8},{11,9},{14,12},{15,13},{18,16},{19,... | collective-permute-start | bytes 1007624 | tf_op jit(solution)/shard_map/ppermute | solution.py:191
